TPU v7x, 256 devices: a whole 4x4x8 slice. The times are simulated.
256 devices in a mesh: vocab: 64 (over y, z, core), token: 4 (over x).
Axes of the slice: x: 4, y: 4, z: 8, core: 2. Of those that a mesh axis runs over, the one named last changes fastest.
Arguments:
- hidden: bfloat16 [32768, 4096], P(('vocab', 'token')), may hold values from -16 to 16
- cand_embed: bfloat16 [8192, 4096], P('vocab'), may hold values from -0.5 to 0.5
- freq_embed: bfloat16 [256, 4096], P('vocab'), may hold values from -0.09375 to 0.09375
- owner_order: int32 [64], replicated, may hold values from 0 to 63, each once
- cand_blocks: int32 [4096, 4], P(('vocab', 'token')), may hold values from 0 to 63, all different within a row; in each aligned block of 16 rows (0 to 15, 16 to 31, ...) at most 2 rows name the same one
- group_tokens: int32 [256, 128], P(('vocab', 'token')), may hold values from 0 to 127, each once within a row
- target_slot: int32 [32768], P(('vocab', 'token')), may hold values from 0 to 767
Outputs:
- logits: bfloat16 [32768, 768], P(('vocab', 'token'))
- loss: float32 [32768], P(('vocab', 'token'))
- grad_hidden: bfloat16 [32768, 4096], P(('vocab', 'token'))
- grad_cand: float32 [8192, 4096], P(('vocab', 'token'))
- grad_freq: float32 [256, 4096], P(('vocab', 'token'))
Inputs may be any that keep to these rules, and one draw needn't show every extreme that they name: `cand_blocks`: each row names 4 different blocks. Among the 16 groups of one device no block is named by more than 2 groups, and some device reaches 2. `group_tokens`: each row lists every number below 128 once. `owner_order`: every number below 64 once.
All inputs are finite; a program needn't handle non-finite values.
Results may differ from a plain program's by a relative error of at most 0.0052.
Values may be sent and summed in bfloat16 or wider, within the bound.
No kernel may reach another device: no remote copies, remote signals or barrier semaphores. Data moves between devices by JAX's collectives and lax.ppermute only.
A program may use at most 128 MiB of HBM per device.

v0:
```python
import jax
import jax.numpy as jnp
from jax import lax
from jax.sharding import PartitionSpec as P

D = 4096
BW = 128
K = 4
GTOK = 8
PANEL = 4
G_DEV = 16


def per_device(hidden, cand_embed, freq_embed, owner_order, cand_blocks, group_tokens, target_slot):
    owners_count = lax.axis_size("vocab")
    token_total = hidden.shape[0]
    freq_count = owners_count * PANEL
    capacity = 2 * G_DEV * K // owners_count
    slot_count = owners_count * capacity
    requests = G_DEV * K
    listing = group_tokens[0]
    grouped = hidden[listing]
    targets = target_slot[listing]
    panels = lax.all_gather(freq_embed, "vocab", axis=0, tiled=True)
    freq_table = panels.reshape(owners_count, PANEL, D)[owner_order].reshape(freq_count, D)
    owner_of = cand_blocks.reshape(requests)
    owner_hot = (owner_of[:, None] == jnp.arange(owners_count, dtype=jnp.int32)[None, :]).astype(
        jnp.int32
    )
    ranking = jnp.sum(jnp.cumsum(owner_hot, axis=0) * owner_hot, axis=1) - 1
    landing = owner_of * capacity + ranking
    placed = (landing[None, :] == jnp.arange(slot_count, dtype=jnp.int32)[:, None]).astype(
        jnp.int32
    )
    occupied = jnp.sum(placed, axis=1)
    request_of = jnp.sum(placed * jnp.arange(requests, dtype=jnp.int32)[None, :], axis=1)
    group_of = request_of // K
    block_rank = request_of % K
    group_rows = grouped.reshape(G_DEV, GTOK, D)
    slot_mask = occupied.astype(jnp.bfloat16)[:, None, None]
    send_rows = (group_rows[group_of] * slot_mask).reshape(owners_count, capacity, GTOK, D)
    group_targets = targets.reshape(G_DEV, GTOK)
    column = group_targets[group_of] - freq_count - block_rank[:, None] * BW
    inside = (column >= 0) & (column < BW) & (occupied[:, None] > 0)
    send_column = jnp.where(inside, column, -1).reshape(owners_count, capacity, GTOK)
    got_rows, got_column = (
        lax.all_to_all(send_rows, "vocab", split_axis=0, concat_axis=0, tiled=True),
        lax.all_to_all(send_column, "vocab", split_axis=0, concat_axis=0, tiled=True),
    )
    scores_here = jnp.einsum(
        "scqd,wd->scqw", got_rows, cand_embed, preferred_element_type=jnp.float32
    )
    scores_home = lax.all_to_all(scores_here, "vocab", split_axis=0, concat_axis=0, tiled=True)
    returned = scores_home.reshape(slot_count, GTOK, BW)[landing]
    cand_scores = (
        returned.reshape(G_DEV, K, GTOK, BW).transpose(0, 2, 1, 3).reshape(token_total, K * BW)
    )
    freq_scores = jnp.einsum("td,fd->tf", grouped, freq_table, preferred_element_type=jnp.float32)
    all_scores = jnp.concatenate([freq_scores, cand_scores], axis=1)
    row_top = jnp.max(all_scores, axis=1)
    exponentials = jnp.exp(all_scores - row_top[:, None])
    total = jnp.sum(exponentials, axis=1)
    inverse_total = 1.0 / total
    columns = jnp.arange(all_scores.shape[1], dtype=jnp.int32)
    target_hot = (targets[:, None] == columns[None, :]).astype(jnp.float32)
    token_loss = jnp.log(total) + row_top - jnp.sum(target_hot * all_scores, axis=1)
    prob_freq = (
        exponentials[:, :freq_count] * inverse_total[:, None] - target_hot[:, :freq_count]
    ).astype(jnp.bfloat16)
    slot_live = occupied[:, None].astype(jnp.float32)
    send_scale = (inverse_total.reshape(G_DEV, GTOK)[group_of] * slot_live).reshape(
        owners_count, capacity, GTOK
    )
    send_top = (row_top.reshape(G_DEV, GTOK)[group_of] * slot_live).reshape(
        owners_count, capacity, GTOK
    )
    got_scale, got_top = (
        lax.all_to_all(send_scale, "vocab", split_axis=0, concat_axis=0, tiled=True),
        lax.all_to_all(send_top, "vocab", split_axis=0, concat_axis=0, tiled=True),
    )
    word_index = jnp.arange(BW, dtype=jnp.int32)
    is_target = (got_column[..., None] == word_index).astype(jnp.float32)
    prob_here = (
        jnp.exp(scores_here - got_top[..., None]) * got_scale[..., None] - is_target
    ).astype(jnp.bfloat16)
    hidden_part = jnp.einsum(
        "scqw,wd->scqd", prob_here, cand_embed, preferred_element_type=jnp.float32
    ).astype(jnp.bfloat16)
    parts_home = lax.all_to_all(hidden_part, "vocab", split_axis=0, concat_axis=0, tiled=True)
    window = prob_here
    grad_cand = lax.psum_scatter(
        jnp.einsum("scqw,scqd->wd", window, got_rows, preferred_element_type=jnp.float32),
        "token",
        scatter_dimension=0,
        tiled=True,
    )
    part_rows = parts_home.reshape(slot_count, GTOK, D)[landing].reshape(G_DEV, K, GTOK, D)
    freq_part = jnp.dot(prob_freq, freq_table, preferred_element_type=jnp.float32)
    grad_rows = freq_part + jnp.sum(part_rows, axis=1, dtype=jnp.float32).reshape(token_total, D)
    position_of = (
        jnp.zeros((owners_count,), jnp.int32)
        .at[owner_order]
        .set(jnp.arange(owners_count, dtype=jnp.int32))
    )
    embed_columns = (
        position_of[:, None] * PANEL + jnp.arange(PANEL, dtype=jnp.int32)[None, :]
    ).reshape(freq_count)
    prob_embed = prob_freq[:, embed_columns]
    window = prob_embed
    grad_freq = lax.psum_scatter(
        jnp.einsum("tf,td->fd", window, grouped, preferred_element_type=jnp.float32),
        ("vocab", "token"),
        scatter_dimension=0,
        tiled=True,
    )
    undo = (
        jnp.zeros((token_total,), jnp.int32)
        .at[listing]
        .set(jnp.arange(token_total, dtype=jnp.int32))
    )
    logits = all_scores.astype(jnp.bfloat16)[undo]
    loss = token_loss[undo]
    grad_hidden = grad_rows.astype(jnp.bfloat16)[undo]
    return (logits, loss, grad_hidden, grad_cand, grad_freq)


def solution(mesh):
    in_specs = (
        P(("vocab", "token"), None),
        P("vocab", None),
        P("vocab", None),
        P(),
        P(("vocab", "token"), None),
        P(("vocab", "token"), None),
        P(("vocab", "token")),
    )
    out_specs = (
        P(("vocab", "token"), None),
        P(("vocab", "token")),
        P(("vocab", "token"), None),
        P(("vocab", "token"), None),
        P(("vocab", "token"), None),
    )
    return jax.shard_map(
        per_device, mesh=mesh, in_specs=in_specs, out_specs=out_specs, check_vma=False
    )
```

profile of v0, /device:TPU:1, one launch (start us, length us, event | category | flops | bytes accessed | tf_op | source)
XLA Modules:
  0.0 685.6 jit_solution(466131606414593907)
XLA Ops:
  7.2 0.7 fusion.16
  7.9 0.8 copy.27
  8.7 0.1 reshape.297
  8.8 0.1 fusion.15
  8.9 0.1 reduce_window_sum.11
  9.0 0.2 select_reduce_fusion.2
  9.2 0.1 convert_reduce_fusion.1
  9.3 0.1 convert_element_type.55
  9.4 3.6 gather_fusion
  13.0 6.4 gather_fusion.2
  19.5 7.3 %broadcast_multiply_fusion = bf16[64,2,8,4096]{3,2,1,0:T(8,128)(2,1)} fusion(bf16[64,2,8,4096]{3,2,1,0:T(8,128)(2,1)} %bitcast.63, bf16[64,2]{1,0:T(8,128)(2,1)S(1)} %convert_element_type.55), kind=kLoop, calls=%fused_computation.22 | loop fusion | flops 4194304 | bytes 16777472 | tf_op jit(solution)/shard_map/mul | solution.py:41
  26.7 13.4 %all-to-all-start = ((bf16[64,2,8,4096]{3,2,1,0:T(8,128)(2,1)}), bf16[64,2,8,4096]{3,2,1,0:T(8,128)(2,1)}, u32[]{:S(2)}, u32[]{:S(2)}) async-start(bf16[64,2,8,4096]{3,2,1,0:T(8,128)(2,1)} %broadcast_multiply_fusion), calls=%async_computation | async-start | bytes 16777216 | tf_op jit(solution)/shard_map/all_to_all | solution.py:47
  40.2 0.7 all-gather.3.cloned.1.call-update
  40.9 0.1 copy.28
  41.0 0.1 mul.104
  41.2 190.9 %all-to-all-done = bf16[64,2,8,4096]{3,2,1,0:T(8,128)(2,1)} async-done(((bf16[64,2,8,4096]{3,2,1,0:T(8,128)(2,1)}), bf16[64,2,8,4096]{3,2,1,0:T(8,128)(2,1)}, u32[]{:S(2)}, u32[]{:S(2)}) %all-to-all-start) | async-done | bytes 8388640 | tf_op jit(solution)/shard_map/all_to_all | solution.py:47
  232.1 6.5 fusion.7
  238.6 6.0 all-to-all-start.1
  244.6 0.1 reduce_sum.64
  244.7 1.2 gather_fusion.5
  245.9 0.1 reshape.301
  246.0 0.2 gt.13
  246.2 0.1 convert_element_type.59
  246.3 0.6 gather_fusion.9
  247.0 0.8 and_select_fusion
  247.9 5.2 gather_fusion.1
  253.1 4.0 reshape.295
  257.0 2.5 fusion.25
  259.5 0.1 reduce_max.32
  259.6 2.2 all-to-all-done.1
  261.8 8.1 %all-to-all-start.4 = ((s32[64,2,8]{2,1,0:T(2,128)}), s32[64,2,8]{2,1,0:T(2,128)S(1)}, u32[]{:S(2)}, u32[]{:S(2)}) async-start(s32[64,2,8]{2,1,0:T(2,128)} %and_select_fusion), calls=%async_computation.4 | async-start | bytes 131072 | tf_op jit(solution)/shard_map/all_to_all | solution.py:48
  270.0 0.6 gather_fusion.3
  270.6 0.1 reduce_max.29
  270.7 0.1 reduce_max.30
  270.8 0.6 gather_fusion.7
  271.5 0.2 fusion.23
  271.7 0.1 div.32
  271.8 0.7 gather_fusion.8
  272.5 0.1 broadcast_multiply_fusion.2
  272.6 7.1 %all-to-all-done.4 = s32[64,2,8]{2,1,0:T(2,128)S(1)} async-done(((s32[64,2,8]{2,1,0:T(2,128)}), s32[64,2,8]{2,1,0:T(2,128)S(1)}, u32[]{:S(2)}, u32[]{:S(2)}) %all-to-all-start.4) | async-done | bytes 4128 | tf_op jit(solution)/shard_map/all_to_all | solution.py:48
  279.7 13.6 %all_to_all.30 = f32[64,2,8]{2,1,0:T(2,128)S(1)} all-to-all(f32[64,2,8]{2,1,0:T(2,128)S(1)} %get-tuple-element.10), channel_id=1, replica_groups=mesh['vocab'=64,'token'=4] {'vocab'}, dimensions={0} | all-to-all | bytes 8192 | tf_op jit(solution)/shard_map/all_to_all | solution.py:79
  293.3 13.6 %all_to_all.31 = f32[64,2,8]{2,1,0:T(2,128)S(1)} all-to-all(f32[64,2,8]{2,1,0:T(2,128)S(1)} %get-tuple-element.11), channel_id=1, replica_groups=mesh['vocab'=64,'token'=4] {'vocab'}, dimensions={0} | all-to-all | bytes 8192 | tf_op jit(solution)/shard_map/all_to_all | solution.py:78
  306.9 6.8 convolution_convert_fusion
  313.7 5.5 all-to-all-start.5
  319.3 0.8 scatter_custom_fusion.1
  320.1 0.1 iota_add_fusion
  320.1 0.1 add.155
  320.3 0.1 iota_compare_fusion.1
  320.4 0.1 fusion.12
  320.5 0.1 copy.31
  320.6 0.9 gather_fusion.12
  321.5 2.6 fusion.26
  324.1 0.3 reduce-scatter.2.cloned.1.call-start
  324.4 6.5 fusion.2
  330.9 1.0 scatter_custom_fusion
  332.0 1.5 gather_fusion.4
  333.5 1.7 gather_fusion.6
  335.2 308.0 %all-reduce.3.cloned.1.call-done = f32[256,4096]{1,0:T(8,128)} async-done(((f32[256,4096]{1,0:T(8,128)}), f32[256,4096]{1,0:T(8,128)}) %all-reduce.3.cloned.1.call-update) | async-done | bytes 4194320
  643.3 1.5 constant_dynamic-slice_fusion
  644.8 6.1 gather_fusion.10
  650.9 3.4 convert_reduce_fusion
  654.3 0.5 fusion.5
  654.8 2.2 gather_fusion.11
  657.0 22.1 %reduce-scatter.2.cloned.1.call-done = f32[32,4096]{1,0:T(8,128)} async-done(((f32[128,4096]{1,0:T(8,128)}), f32[32,4096]{1,0:T(8,128)}) %reduce-scatter.2.cloned.1.call-update) | async-done | bytes 524304 | tf_op jit(solution)/shard_map/reduce_scatter | solution.py:91
  (42 shorter events, 0.3 us)
Async XLA Ops:
  7.2 224.9 %copy-start = (bf16[128,4096]{1,0:T(8,128)(2,1)S(1)}, bf16[128,4096]{1,0:T(8,128)(2,1)}, u32[]{:S(2)}) copy-start(bf16[128,4096]{1,0:T(8,128)(2,1)} %param.8) | copy-start | bytes 3145732
  26.7 14.2 %copy-start.4 = (s32[16,4]{0,1:T(4,128)S(1)}, s32[16,4]{0,1:T(4,128)}, u32[]{:S(2)}) copy-start(s32[16,4]{0,1:T(4,128)} %param.11) | copy-start | bytes 772
  26.7 14.4 %copy-start.5 = (s32[64]{0:T(128)S(1)}, s32[64]{0:T(128)}, u32[]{:S(2)}) copy-start(s32[64]{0:T(128)} %param.10) | copy-start | bytes 772
  26.7 205.3 %all-to-all-start = ((bf16[64,2,8,4096]{3,2,1,0:T(8,128)(2,1)}), bf16[64,2,8,4096]{3,2,1,0:T(8,128)(2,1)}, u32[]{:S(2)}, u32[]{:S(2)}) async-start(bf16[64,2,8,4096]{3,2,1,0:T(8,128)(2,1)} %broadcast_multiply_fusion), calls=%async_computation | async-start | bytes 16777216 | tf_op jit(solution)/shard_map/all_to_all | solution.py:47
  40.2 207.7 %all-gather.3.cloned.1.call-start = ((), (), s32[]{:S(2)}) async-start(), calls=%async_computation.8 | async-start | bytes 2129920 | tf_op jit(solution)/shard_map/all_gather | solution.py:24
  41.2 203.5 %copy-start.2 = (s32[128]{0:T(128)S(1)}, s32[128]{0:T(128)}, u32[]{:S(2)}) copy-start(s32[128]{0:T(128)} %param.13) | copy-start | bytes 1540
  238.6 23.3 %all-to-all-start.1 = ((f32[64,2,8,128]{3,2,1,0:T(8,128)}), f32[64,2,8,128]{3,2,1,0:T(8,128)S(1)}, u32[]{:S(2)}, u32[]{:S(2)}) async-start(f32[64,2,8,128]{3,2,1,0:T(8,128)} %fusion.7), calls=%async_computation.1 | async-start | bytes 1048576 | tf_op jit(solution)/shard_map/all_to_all | solution.py:53
  261.8 17.9 %all-to-all-start.4 = ((s32[64,2,8]{2,1,0:T(2,128)}), s32[64,2,8]{2,1,0:T(2,128)S(1)}, u32[]{:S(2)}, u32[]{:S(2)}) async-start(s32[64,2,8]{2,1,0:T(2,128)} %and_select_fusion), calls=%async_computation.4 | async-start | bytes 131072 | tf_op jit(solution)/shard_map/all_to_all | solution.py:48
  313.7 331.1 %all-to-all-start.5 = ((bf16[64,2,8,4096]{3,2,1,0:T(8,128)(2,1)}), bf16[64,2,8,4096]{3,2,1,0:T(8,128)(2,1)}, u32[]{:S(2)}, u32[]{:S(2)}) async-start(bf16[64,2,8,4096]{3,2,1,0:T(8,128)(2,1)} %convolution_convert_fusion), calls=%async_computation.5 | async-start | bytes 16777216 | tf_op jit(solution)/shard_map/all_to_all | solution.py:89
  319.2 324.1 %all-reduce.3.cloned.1.call-start = ((), (), s32[]{:S(2)}) async-start(), calls=%async_computation.9 | async-start | bytes 8388608
  324.1 354.9 %reduce-scatter.2.cloned.1.call-start = ((), (), s32[]{:S(2)}) async-start(), calls=%async_computation.7 | async-start | bytes 2621440 | tf_op jit(solution)/shard_map/reduce_scatter | solution.py:91
  650.9 3.4 copy-start.3
  654.3 24.7 %copy-start.1 = (bf16[128,4096]{1,0:T(8,128)(2,1)S(1)}, bf16[128,4096]{1,0:T(8,128)(2,1)}, u32[]{:S(2)}) copy-start(bf16[128,4096]{1,0:T(8,128)(2,1)} %param.8) | copy-start | bytes 3145732
Sparse Core Ops, SparseCore 0:
  43.8 92.4 all-gather.2
  325.5 317.7 all-reduce.2
  646.4 32.5 reduce-scatter.1
where the time goes:
time: 686 us
  waiting for transfers between devices  531 us (77%)
  local copies, waits for them, and re-layouts  40.8 us (6%)
  starting transfers between devices  33.4 us (5%)
  blocking collectives  27.2 us (4%)
  matrix products  25.3 us (4%)
  between operations  14.2 us (2%)
  other arithmetic  13.6 us (2%)
    unnamed x4, waiting for transfers between devices  309 us
    all_to_all x1, waiting for transfers between devices, per_device(): lax.all_to_all(send_rows, 'vocab', split_axis=0, concat_axis=0, tiled=True)  191 us
    reduce_scatter x1, waiting for transfers between devices, per_device(): lax.psum_scatter(jnp.einsum('scqw,scqd->wd', window, got_rows, preferred_...  22.1 us
  transfers between devices with their start and end apart: 7, of which 5 were waited for; matrix products, arithmetic and copies ran while one was open for 8% of the time, Pallas kernels for 0%

commit v1 on v0

--- a/solution.py
+++ b/solution.py
@@ -43,10 +43,7 @@
     column = group_targets[group_of] - freq_count - block_rank[:, None] * BW
     inside = (column >= 0) & (column < BW) & (occupied[:, None] > 0)
     send_column = jnp.where(inside, column, -1).reshape(owners_count, capacity, GTOK)
-    got_rows, got_column = (
-        lax.all_to_all(send_rows, "vocab", split_axis=0, concat_axis=0, tiled=True),
-        lax.all_to_all(send_column, "vocab", split_axis=0, concat_axis=0, tiled=True),
-    )
+    got_rows = lax.all_to_all(send_rows, "vocab", split_axis=0, concat_axis=0, tiled=True)
     scores_here = jnp.einsum(
         "scqd,wd->scqw", got_rows, cand_embed, preferred_element_type=jnp.float32
     )
@@ -74,10 +71,10 @@
     send_top = (row_top.reshape(G_DEV, GTOK)[group_of] * slot_live).reshape(
         owners_count, capacity, GTOK
     )
-    got_scale, got_top = (
-        lax.all_to_all(send_scale, "vocab", split_axis=0, concat_axis=0, tiled=True),
-        lax.all_to_all(send_top, "vocab", split_axis=0, concat_axis=0, tiled=True),
-    )
+    send_stats = jnp.stack([send_scale, send_top, send_column.astype(jnp.float32)], axis=-1)
+    got_stats = lax.all_to_all(send_stats, "vocab", split_axis=0, concat_axis=0, tiled=True)
+    got_scale, got_top = got_stats[..., 0], got_stats[..., 1]
+    got_column = got_stats[..., 2].astype(jnp.int32)
     word_index = jnp.arange(BW, dtype=jnp.int32)
     is_target = (got_column[..., None] == word_index).astype(jnp.float32)
     prob_here = (
@@ -107,11 +104,12 @@
     ).reshape(freq_count)
     prob_embed = prob_freq[:, embed_columns]
     window = prob_embed
+    token_count = lax.axis_size("token")
+    freq_partial = jnp.einsum("tf,td->fd", window, grouped, preferred_element_type=jnp.float32)
+    freq_partial = freq_partial.reshape(freq_count // token_count, token_count, D).transpose(1, 0, 2)
+    freq_partial = lax.psum_scatter(freq_partial, "token", scatter_dimension=0, tiled=True)
     grad_freq = lax.psum_scatter(
-        jnp.einsum("tf,td->fd", window, grouped, preferred_element_type=jnp.float32),
-        ("vocab", "token"),
-        scatter_dimension=0,
-        tiled=True,
+        freq_partial.reshape(freq_count // token_count, D), "vocab", scatter_dimension=0, tiled=True
     )
     undo = (
         jnp.zeros((token_total,), jnp.int32)

time: 686 us -> 615 us (0.90)
  waiting for transfers between devices: 531 us -> 465 us
  local copies, waits for them, and re-layouts: 40.8 us -> 54.7 us
  blocking collectives: 27.2 us -> 17 us
  starting transfers between devices: 33.4 us -> 25.4 us
    unnamed x4 -> x5, waiting for transfers between devices: 309 us -> 201 us
    reduce_scatter x0 -> x1, waiting for transfers between devices: none -> 50.4 us  [per_device(): lax.psum_scatter(freq_partial, 'token', scatter_dimension=0, tiled=True)]
    reshape x0 -> x2, local copies, waits for them, and re-layouts: none -> 11.7 us  [per_device(): freq_partial.reshape(freq_count // token_count, token_count, D)]
    all_to_all x2 -> x1, blocking collectives: 27.2 us -> 17 us  [per_device(): lax.all_to_all(send_stats, 'vocab', split_axis=0, concat_axis=0, tiled=True)]
    all_to_all x1 -> x0, starting transfers between devices: 8.12 us -> none  [per_device(): lax.all_to_all(send_column, 'vocab', split_axis=0, concat_axis=0, tiled=T...]
    all_to_all x1 -> x0, waiting for transfers between devices: 7.14 us -> none  [per_device(): lax.all_to_all(send_column, 'vocab', split_axis=0, concat_axis=0, tiled=T...]
  transfers between devices with their start and end apart: 7 -> 7, of which waited for: 5 -> 5; matrix products, arithmetic and copies ran while one was open for 8% -> 10% of each run, Pallas kernels for 0% -> 0%
where the time goes in v1:
time: 615 us; the launch traced here: 614 us
  waiting for transfers between devices  465 us (76%)
  local copies, waits for them, and re-layouts  54.7 us (9%)
  starting transfers between devices  25.4 us (4%)
  matrix products  25.4 us (4%)
  blocking collectives  17 us (3%)
  between operations  14.2 us (2%)
  other arithmetic  12.7 us (2%)
    unnamed x5, waiting for transfers between devices  201 us
    all_to_all x1, waiting for transfers between devices, per_device(): lax.all_to_all(send_rows, 'vocab', split_axis=0, concat_axis=0, tiled=True)  189 us
    reduce_scatter x1, waiting for transfers between devices, per_device(): lax.psum_scatter(freq_partial, 'token', scatter_dimension=0, tiled=True)  50.4 us
    reduce_scatter x1, waiting for transfers between devices, per_device(): lax.psum_scatter(jnp.einsum('scqw,scqd->wd', window, got_rows, preferred_...  20.1 us
    all_to_all x1, blocking collectives, per_device(): lax.all_to_all(send_stats, 'vocab', split_axis=0, concat_axis=0, tiled=True)  17 us
    all_to_all x1, starting transfers between devices, per_device(): lax.all_to_all(send_rows, 'vocab', split_axis=0, concat_axis=0, tiled=True)  13.5 us
  transfers between devices with their start and end apart: 7, of which 5 were waited for; matrix products, arithmetic and copies ran while one was open for 10% of the time, Pallas kernels for 0%

profile of v1, /device:TPU:1, one launch (start us, length us, event | category | flops | bytes accessed | tf_op | source)
XLA Modules:
  0.0 614.3 jit_solution(15391265597055532244)
XLA Ops:
  7.2 0.7 fusion.17
  7.9 0.8 copy.50
  8.7 0.1 reshape.351
  8.8 0.1 fusion.14
  8.9 0.1 reduce_window_sum.11
  9.0 0.2 select_reduce_fusion.2
  9.2 0.1 convert_reduce_fusion.1
  9.3 0.1 convert_element_type.69
  9.4 3.6 gather_fusion
  13.0 6.4 %gather_fusion.2 = bf16[128,8,4096]{2,1,0:T(8,128)(2,1)} fusion(bf16[16,8,4096]{2,1,0:T(8,128)(2,1)S(1)} %bitcast.73, s32[1024]{0:T(1024)S(1)} %pad_clamp_fusion.3), kind=kCustom, calls=%fused_computation.2 | custom fusion | bytes 16777728 | tf_op jit(solution)/shard_map/gather | solution.py:41
  19.5 7.3 %broadcast_multiply_fusion = bf16[64,2,8,4096]{3,2,1,0:T(8,128)(2,1)} fusion(bf16[64,2,8,4096]{3,2,1,0:T(8,128)(2,1)} %bitcast.74, bf16[64,2]{1,0:T(8,128)(2,1)S(1)} %convert_element_type.69), kind=kLoop, calls=%fused_computation.23 | loop fusion | flops 4194304 | bytes 16777472 | tf_op jit(solution)/shard_map/mul | solution.py:41
  26.7 13.5 %all-to-all-start = ((bf16[64,2,8,4096]{3,2,1,0:T(8,128)(2,1)}), bf16[64,2,8,4096]{3,2,1,0:T(8,128)(2,1)}, u32[]{:S(2)}, u32[]{:S(2)}) async-start(bf16[64,2,8,4096]{3,2,1,0:T(8,128)(2,1)} %broadcast_multiply_fusion), calls=%async_computation | async-start | bytes 16777216 | tf_op jit(solution)/shard_map/all_to_all | solution.py:46
  40.2 0.7 all-gather.3.cloned.1.call-update
  40.9 1.2 gather_fusion.5
  42.2 0.1 copy.51
  42.3 0.1 mul.118
  42.4 0.1 reshape.355
  42.4 0.7 gather_fusion.9
  43.1 188.9 %all-to-all-done = bf16[64,2,8,4096]{3,2,1,0:T(8,128)(2,1)} async-done(((bf16[64,2,8,4096]{3,2,1,0:T(8,128)(2,1)}), bf16[64,2,8,4096]{3,2,1,0:T(8,128)(2,1)}, u32[]{:S(2)}, u32[]{:S(2)}) %all-to-all-start) | async-done | bytes 8388640 | tf_op jit(solution)/shard_map/all_to_all | solution.py:46
  232.1 6.5 %fusion.7 = f32[64,2,8,128]{3,2,1,0:T(8,128)} fusion(bf16[64,2,8,4096]{3,2,1,0:T(8,128)(2,1)} %all-to-all-done, bf16[128,4096]{1,0:T(8,128)(2,1)S(1)} %copy-done), kind=kOutput, calls=%fused_computation.25 | convolution fusion | flops 1073741824 | bytes 9961472 | tf_op jit(solution)/shard_map/scqd,wd->scqw/dot_general | solution.py:47
  238.6 6.0 all-to-all-start.1
  244.6 0.1 reduce_sum.64
  244.7 0.2 gt.13
  244.9 0.1 copy.59
  245.0 0.1 convert_element_type.73
  245.3 0.1 copy.58
  245.4 5.2 gather_fusion.1
  250.6 4.0 reshape.349
  254.6 2.5 fusion.26
  257.1 0.1 reduce_max.32
  257.2 4.7 all-to-all-done.1
  261.8 0.6 gather_fusion.3
  262.5 0.1 reduce_max.29
  262.6 0.1 reduce_max.30
  262.7 0.6 gather_fusion.8
  263.4 0.3 fusion.24
  263.7 0.1 div.32
  263.8 0.7 gather_fusion.7
  264.5 0.2 copy.60
  264.7 17.0 %all_to_all.20 = f32[64,2,8,3]{2,1,3,0:T(2,128)S(1)} all-to-all(f32[64,2,8,3]{2,1,3,0:T(2,128)S(1)} %copy.60), channel_id=1, replica_groups=mesh['vocab'=64,'token'=4] {'vocab'}, dimensions={0} | all-to-all | bytes 24576 | tf_op jit(solution)/shard_map/all_to_all | solution.py:75
  281.8 6.8 %convolution_convert_fusion = bf16[64,2,8,4096]{3,2,1,0:T(8,128)(2,1)} fusion(bf16[128,4096]{1,0:T(8,128)(2,1)S(1)} %copy-done, f32[64,2,8,128]{3,2,1,0:T(8,128)} %fusion.7, s32[64,2,8]{2,1,0:T(2,128)S(1)} %get-tuple-element.11, f32[64,2,8]{2,1,0:T(2,128)S(1)} %get-tuple-element.12, f32[64,2,8]{2,1,0:T(2,128)S(1)} %get-tuple-element.10), kind=kOutput, calls=%fused_computation.18 | convolution fusion | flops 1078722560 | bytes 9973760 | tf_op jit(solution)/shard_map/scqw,wd->scqd/dot_general | solution.py:83
  288.6 5.8 all-to-all-start.3
  294.5 1.0 scatter_custom_fusion.1
  295.6 0.1 add.164
  295.7 0.1 iota_compare_fusion.1
  295.8 0.1 fusion.12
  295.9 0.1 copy.63
  296.0 0.9 gather_fusion.12
  296.9 2.6 fusion.27
  299.5 5.2 reshape.358
  304.7 6.6 %copy.74 = f32[64,4,4096]{2,0,1:T(8,128)} copy(f32[64,4,4096]{2,1,0:T(4,128)} %reshape.358) | data formatting | bytes 8388608 | tf_op jit(solution)/shard_map/reshape | solution.py:109
  311.3 50.4 %reduce-scatter.5.cloned.1.call-done = f32[1,64,4096]{2,1,0:T(8,128)} async-done(((f32[4,64,4096]{2,1,0:T(8,128)}), f32[1,64,4096]{2,1,0:T(8,128)}) %reduce-scatter.5.cloned.1.call-update) | async-done | bytes 1048592 | tf_op jit(solution)/shard_map/reduce_scatter | solution.py:110
  361.8 6.5 %fusion.2 = f32[128,4096]{1,0:T(8,128)} fusion(bf16[64,2,8,4096]{3,2,1,0:T(8,128)(2,1)} %all-to-all-done, f32[64,2,8,128]{3,2,1,0:T(8,128)} %fusion.7, s32[64,2,8]{2,1,0:T(2,128)S(1)} %get-tuple-element.11, f32[64,2,8]{2,1,0:T(2,128)S(1)} %get-tuple-element.12, f32[64,2,8]{2,1,0:T(2,128)S(1)} %get-tuple-element.10), kind=kOutput, calls=%fused_computation.19 | convolution fusion | flops 1074528256 | bytes 11022336 | tf_op jit(solution)/shard_map/scqw,scqd->wd/dot_general | solution.py:89
  368.3 1.0 scatter_custom_fusion
  369.3 0.6 dynamic-slice
  370.0 1.5 gather_fusion.4
  371.5 1.7 gather_fusion.6
  373.2 200.1 %all-reduce.3.cloned.1.call-done = f32[64,4096]{1,0:T(8,128)} async-done(((f32[64,4096]{1,0:T(8,128)}), f32[64,4096]{1,0:T(8,128)}) %all-reduce.3.cloned.1.call-update) | async-done | bytes 1048592
  573.4 2.2 constant_dynamic-slice_fusion
  575.6 6.1 gather_fusion.10
  581.7 3.4 convert_reduce_fusion
  585.1 0.5 fusion.5
  585.5 2.2 gather_fusion.11
  587.7 20.1 %reduce-scatter.3.cloned.1.call-done = f32[32,4096]{1,0:T(8,128)} async-done(((f32[128,4096]{1,0:T(8,128)}), f32[32,4096]{1,0:T(8,128)}) %reduce-scatter.3.cloned.1.call-update) | async-done | bytes 524304 | tf_op jit(solution)/shard_map/reduce_scatter | solution.py:88
  (56 shorter events, 0.9 us)
Async XLA Ops:
  7.2 224.9 %copy-start = (bf16[128,4096]{1,0:T(8,128)(2,1)S(1)}, bf16[128,4096]{1,0:T(8,128)(2,1)}, u32[]{:S(2)}) copy-start(bf16[128,4096]{1,0:T(8,128)(2,1)} %param.8) | copy-start | bytes 3145732
  26.7 14.2 %copy-start.2 = (s32[128]{0:T(128)S(1)}, s32[128]{0:T(128)}, u32[]{:S(2)}) copy-start(s32[128]{0:T(128)} %param.13) | copy-start | bytes 1540
  26.7 15.4 %copy-start.4 = (s32[16,4]{0,1:T(4,128)S(1)}, s32[16,4]{0,1:T(4,128)}, u32[]{:S(2)}) copy-start(s32[16,4]{0,1:T(4,128)} %param.11) | copy-start | bytes 772
  26.7 205.3 %all-to-all-start = ((bf16[64,2,8,4096]{3,2,1,0:T(8,128)(2,1)}), bf16[64,2,8,4096]{3,2,1,0:T(8,128)(2,1)}, u32[]{:S(2)}, u32[]{:S(2)}) async-start(bf16[64,2,8,4096]{3,2,1,0:T(8,128)(2,1)} %broadcast_multiply_fusion), calls=%async_computation | async-start | bytes 16777216 | tf_op jit(solution)/shard_map/all_to_all | solution.py:46
  40.2 205.3 %all-gather.3.cloned.1.call-start = ((), (), s32[]{:S(2)}) async-start(), calls=%async_computation.8 | async-start | bytes 2129920 | tf_op jit(solution)/shard_map/all_gather | solution.py:24
  43.1 201.4 %copy-start.5 = (s32[64]{0:T(128)S(1)}, s32[64]{0:T(128)}, u32[]{:S(2)}) copy-start(s32[64]{0:T(128)} %param.10) | copy-start | bytes 772
  238.6 23.3 %all-to-all-start.1 = ((f32[64,2,8,128]{3,2,1,0:T(8,128)}), f32[64,2,8,128]{3,2,1,0:T(8,128)S(1)}, u32[]{:S(2)}, u32[]{:S(2)}) async-start(f32[64,2,8,128]{3,2,1,0:T(8,128)} %fusion.7), calls=%async_computation.1 | async-start | bytes 1048576 | tf_op jit(solution)/shard_map/all_to_all | solution.py:50
  288.6 287.0 %all-to-all-start.3 = ((bf16[64,2,8,4096]{3,2,1,0:T(8,128)(2,1)}), bf16[64,2,8,4096]{3,2,1,0:T(8,128)(2,1)}, u32[]{:S(2)}, u32[]{:S(2)}) async-start(bf16[64,2,8,4096]{3,2,1,0:T(8,128)(2,1)} %convolution_convert_fusion), calls=%async_computation.3 | async-start | bytes 16777216 | tf_op jit(solution)/shard_map/all_to_all | solution.py:86
  294.4 67.3 %reduce-scatter.5.cloned.1.call-start = ((), (), s32[]{:S(2)}) async-start(), calls=%async_computation.7 | async-start | bytes 5242880 | tf_op jit(solution)/shard_map/reduce_scatter | solution.py:110
  311.3 262.1 %all-reduce.3.cloned.1.call-start = ((), (), s32[]{:S(2)}) async-start(), calls=%async_computation.9 | async-start | bytes 2097152
  361.8 7.6 %copy-start.6 = (u32[256]{0:T(256)S(1)}, u32[256]{0:T(256)}, u32[]{:S(2)}) copy-start(u32[256]{0:T(256)} %constant.72) | copy-start | bytes 3076
  361.8 246.0 %reduce-scatter.3.cloned.1.call-start = ((), (), s32[]{:S(2)}) async-start(), calls=%async_computation.6 | async-start | bytes 2621440 | tf_op jit(solution)/shard_map/reduce_scatter | solution.py:88
  581.7 3.4 copy-start.3
  585.1 22.7 %copy-start.1 = (bf16[128,4096]{1,0:T(8,128)(2,1)S(1)}, bf16[128,4096]{1,0:T(8,128)(2,1)}, u32[]{:S(2)}) copy-start(bf16[128,4096]{1,0:T(8,128)(2,1)} %param.8) | copy-start | bytes 3145732
Sparse Core Ops, SparseCore 0:
  43.8 92.5 all-gather.2
  311.4 50.2 reduce-scatter.4
  365.2 208.1 all-reduce.2
  576.4 31.3 reduce-scatter.2

commit v2 on v1

--- a/solution.py
+++ b/solution.py
@@ -36,9 +36,7 @@
     request_of = jnp.sum(placed * jnp.arange(requests, dtype=jnp.int32)[None, :], axis=1)
     group_of = request_of // K
     block_rank = request_of % K
-    group_rows = grouped.reshape(G_DEV, GTOK, D)
-    slot_mask = occupied.astype(jnp.bfloat16)[:, None, None]
-    send_rows = (group_rows[group_of] * slot_mask).reshape(owners_count, capacity, GTOK, D)
+    send_rows = hidden[listing.reshape(G_DEV, GTOK)[group_of]].reshape(owners_count, capacity, GTOK, D)
     group_targets = targets.reshape(G_DEV, GTOK)
     column = group_targets[group_of] - freq_count - block_rank[:, None] * BW
     inside = (column >= 0) & (column < BW) & (occupied[:, None] > 0)
@@ -77,8 +75,10 @@
     got_column = got_stats[..., 2].astype(jnp.int32)
     word_index = jnp.arange(BW, dtype=jnp.int32)
     is_target = (got_column[..., None] == word_index).astype(jnp.float32)
+    live_here = got_scale[..., None] > 0
     prob_here = (
-        jnp.exp(scores_here - got_top[..., None]) * got_scale[..., None] - is_target
+        jnp.where(live_here, jnp.exp(scores_here - got_top[..., None]) * got_scale[..., None], 0.0)
+        - is_target
     ).astype(jnp.bfloat16)
     hidden_part = jnp.einsum(
         "scqw,wd->scqd", prob_here, cand_embed, preferred_element_type=jnp.float32
@@ -108,9 +108,10 @@
     freq_partial = jnp.einsum("tf,td->fd", window, grouped, preferred_element_type=jnp.float32)
     freq_partial = freq_partial.reshape(freq_count // token_count, token_count, D).transpose(1, 0, 2)
     freq_partial = lax.psum_scatter(freq_partial, "token", scatter_dimension=0, tiled=True)
-    grad_freq = lax.psum_scatter(
-        freq_partial.reshape(freq_count // token_count, D), "vocab", scatter_dimension=0, tiled=True
+    freq_pieces = lax.all_to_all(
+        freq_partial.reshape(freq_count // token_count, D), "vocab", split_axis=0, concat_axis=0, tiled=True
     )
+    grad_freq = jnp.sum(freq_pieces, axis=0, keepdims=True)
     undo = (
         jnp.zeros((token_total,), jnp.int32)
         .at[listing]

time: 615 us -> 574 us (0.933)
  waiting for transfers between devices: 465 us -> 427 us
  starting transfers between devices: 25.4 us -> 43.4 us
  blocking collectives: 17 us -> 0 us
    unnamed x5 -> x3, waiting for transfers between devices: 201 us -> 0.71 us
    all_to_all x1, waiting for transfers between devices: 0.01 us -> 173 us  [per_device(): lax.all_to_all(hidden_part, 'vocab', split_axis=0, concat_axis=0, tiled=T...]
    all_to_all x0 -> x2, waiting for transfers between devices: none -> 22.6 us  [the longest x1 22.6 us: per_device(): lax.all_to_all(freq_partial.reshape(freq_count // token_count, D), 'vocab...]
    reduce_scatter x1, waiting for transfers between devices: 20.1 us -> 0.01 us  [per_device(): lax.psum_scatter(jnp.einsum('scqw,scqd->wd', window, got_rows, preferred_...]
    all_to_all x0 -> x2, starting transfers between devices: none -> 17.1 us  [the longest x1 10.8 us: per_device(): lax.all_to_all(freq_partial.reshape(freq_count // token_count, D), 'vocab...]
    all_to_all x1 -> x0, blocking collectives: 17 us -> none  [per_device(): lax.all_to_all(send_stats, 'vocab', split_axis=0, concat_axis=0, tiled=True)]
    reduce_scatter x1, waiting for transfers between devices: 50.4 us -> 36.1 us  [per_device(): lax.psum_scatter(freq_partial, 'token', scatter_dimension=0, tiled=True)]
    mul x1 -> x0, other arithmetic: 7.25 us -> none  [per_device(): group_rows[group_of] * slot_mask]
  transfers between devices with their start and end apart: 7 -> 8, of which waited for: 5 -> 5; matrix products, arithmetic and copies ran while one was open for 10% -> 10% of each run, Pallas kernels for 0% -> 0%
where the time goes in v2:
time: 574 us; the launch traced here: 573 us
  waiting for transfers between devices  427 us (74%)
  local copies, waits for them, and re-layouts  56.5 us (10%)
  starting transfers between devices  43.4 us (8%)
  matrix products  24 us (4%)
  between operations  14.3 us (2%)
  other arithmetic  7.67 us (1%)
    all_to_all x1, waiting for transfers between devices, per_device(): lax.all_to_all(send_rows, 'vocab', split_axis=0, concat_axis=0, tiled=True)  190 us
    all_to_all x1, waiting for transfers between devices, per_device(): lax.all_to_all(hidden_part, 'vocab', split_axis=0, concat_axis=0, tiled=T...  173 us
    reduce_scatter x1, waiting for transfers between devices, per_device(): lax.psum_scatter(freq_partial, 'token', scatter_dimension=0, tiled=True)  36.1 us
    all_to_all x1, waiting for transfers between devices, per_device(): lax.all_to_all(freq_partial.reshape(freq_count // token_count, D), 'vocab...  22.6 us
    all_to_all x1, starting transfers between devices, per_device(): lax.all_to_all(send_rows, 'vocab', split_axis=0, concat_axis=0, tiled=True)  13.5 us
    reshape x2, local copies, waits for them, and re-layouts, per_device(): freq_partial.reshape(freq_count // token_count, token_count, D)  11.8 us
  transfers between devices with their start and end apart: 8, of which 5 were waited for; matrix products, arithmetic and copies ran while one was open for 10% of the time, Pallas kernels for 0%

profile of v2, /device:TPU:1, one launch (start us, length us, event | category | flops | bytes accessed | tf_op | source)
XLA Modules:
  0.0 572.9 jit_solution(13156015347748647646)
XLA Ops:
  7.2 0.5 broadcast.410
  7.7 1.3 reduce.7
  9.0 0.1 reshape_squeeze.3
  9.1 0.8 copy.63
  9.9 0.1 reshape.355
  10.0 0.1 reduce_window_sum.11
  10.1 0.2 select_reduce_fusion.2
  10.3 0.1 convert_reduce_fusion.1
  10.5 0.6 gather_fusion.2
  11.1 0.1 reshape.391
  11.2 7.8 %gather_fusion.3 = bf16[1024,4096]{1,0:T(8,128)(2,1)} fusion(bf16[128,4096]{1,0:T(8,128)(2,1)S(1)} %copy-done, s32[1024]{0:T(1024)S(1)} %broadcast_clamp_fusion), kind=kCustom, calls=%fused_computation.3 | custom fusion | bytes 16781312 | tf_op jit(solution)/shard_map/gather | solution.py:39
  19.1 13.5 %all-to-all-start = ((bf16[64,2,8,4096]{3,2,1,0:T(8,128)(2,1)}), bf16[64,2,8,4096]{3,2,1,0:T(8,128)(2,1)}, u32[]{:S(2)}, u32[]{:S(2)}) async-start(bf16[64,2,8,4096]{3,2,1,0:T(8,128)(2,1)} %bitcast.78), calls=%async_computation | async-start | bytes 16777216 | tf_op jit(solution)/shard_map/all_to_all | solution.py:44
  32.6 0.7 all-gather.3.cloned.1.call-update
  33.3 0.8 scatter_custom_fusion.1
  34.2 0.1 add.173
  34.4 190.1 %all-to-all-done = bf16[64,2,8,4096]{3,2,1,0:T(8,128)(2,1)} async-done(((bf16[64,2,8,4096]{3,2,1,0:T(8,128)(2,1)}), bf16[64,2,8,4096]{3,2,1,0:T(8,128)(2,1)}, u32[]{:S(2)}, u32[]{:S(2)}) %all-to-all-start) | async-done | bytes 8388640 | tf_op jit(solution)/shard_map/all_to_all | solution.py:44
  224.4 6.5 %fusion.7 = f32[64,2,8,128]{3,2,1,0:T(8,128)} fusion(bf16[64,2,8,4096]{3,2,1,0:T(8,128)(2,1)} %all-to-all-done, bf16[128,4096]{1,0:T(8,128)(2,1)S(1)} %copy-done.6), kind=kOutput, calls=%fused_computation.25 | convolution fusion | flops 1073741824 | bytes 9961472 | tf_op jit(solution)/shard_map/scqd,wd->scqw/dot_general | solution.py:45
  230.9 6.2 %all-to-all-start.1 = ((f32[64,2,8,128]{3,2,1,0:T(8,128)}), f32[64,2,8,128]{3,2,1,0:T(8,128)}, u32[]{:S(2)}, u32[]{:S(2)}) async-start(f32[64,2,8,128]{3,2,1,0:T(8,128)} %fusion.7), calls=%async_computation.1 | async-start | bytes 1048576 | tf_op jit(solution)/shard_map/all_to_all | solution.py:48
  237.1 0.2 reduce-scatter.5.cloned.1.call-start
  237.4 2.2 gather_fusion
  239.5 1.2 gather_fusion.6
  240.8 0.1 copy.64
  240.9 0.1 mul.107
  241.0 0.1 iota_compare_fusion.1
  241.2 5.3 gather_fusion.1
  246.4 2.5 reshape.354
  249.0 0.9 fusion.25
  249.9 4.4 all-to-all-done.1
  254.3 1.6 gather_fusion.4
  256.0 0.1 reduce_max.29
  256.1 0.1 reduce_max.30
  256.2 0.3 fusion.24
  256.4 0.1 fusion.12
  256.5 0.1 copy.76
  256.6 0.9 gather_fusion.13
  257.5 3.9 fusion.26
  261.4 5.2 reshape.363
  266.6 6.6 %copy.88 = f32[64,4,4096]{2,0,1:T(8,128)} copy(f32[64,4,4096]{2,1,0:T(4,128)} %reshape.363) | data formatting | bytes 8388608 | tf_op jit(solution)/shard_map/reshape | solution.py:109
  273.3 0.1 reduce_sum.73
  273.4 0.1 gt.19
  273.6 0.1 copy.72
  273.7 0.2 convert_element_type.61
  274.0 0.7 gather_fusion.10
  274.8 0.1 div.32
  274.9 0.6 gather_fusion.9
  275.7 0.7 gather_fusion.8
  276.4 0.8 copy.73
  277.2 6.3 %all-to-all-start.2 = ((f32[64,2,8,3]{2,1,3,0:T(2,128)}), f32[64,2,8,3]{2,1,3,0:T(2,128)S(1)}, u32[]{:S(2)}, u32[]{:S(2)}) async-start(f32[64,2,8,3]{2,1,3,0:T(2,128)} %copy.73), calls=%async_computation.2 | async-start | bytes 393216 | tf_op jit(solution)/shard_map/all_to_all | solution.py:73
  283.5 36.1 %reduce-scatter.5.cloned.1.call-done = f32[1,64,4096]{2,1,0:T(8,128)} async-done(((f32[4,64,4096]{2,1,0:T(8,128)}), f32[1,64,4096]{2,1,0:T(8,128)}) %reduce-scatter.5.cloned.1.call-update) | async-done | bytes 1048592 | tf_op jit(solution)/shard_map/reduce_scatter | solution.py:110
  319.5 3.3 copy.78
  322.8 10.8 %all-to-all-start.4 = ((f32[64,1,4096]{2,1,0:T(1,128)}), f32[64,1,4096]{2,1,0:T(1,128)S(1)}, u32[]{:S(2)}, u32[]{:S(2)}) async-start(f32[64,1,4096]{2,1,0:T(1,128)} %copy.78), calls=%async_computation.6 | async-start | bytes 2097152 | tf_op jit(solution)/shard_map/all_to_all | solution.py:111
  333.7 5.8 %convolution_convert_fusion = bf16[64,2,8,4096]{3,2,1,0:T(8,128)(2,1)} fusion(bf16[128,4096]{1,0:T(8,128)(2,1)S(1)} %copy-done.7, f32[64,2,8,128]{3,2,1,0:T(8,128)} %fusion.7, s32[64,2,8]{2,1,0:T(2,128)S(1)} %get-tuple-element.12, f32[64,2,8]{2,1,0:T(2,128)S(1)} %get-tuple-element.11, f32[64,2,8]{2,1,0:T(2,128)S(1)} %get-tuple-element.10, ...), kind=kOutput, calls=%fused_computation.19 | convolution fusion | flops 1078853632 | bytes 9974784 | tf_op jit(solution)/shard_map/scqw,wd->scqd/dot_general | solution.py:83
  339.5 22.6 %all-to-all-done.4 = f32[64,1,4096]{2,1,0:T(1,128)S(1)} async-done(((f32[64,1,4096]{2,1,0:T(1,128)}), f32[64,1,4096]{2,1,0:T(1,128)S(1)}, u32[]{:S(2)}, u32[]{:S(2)}) %all-to-all-start.4) | async-done | bytes 1048608 | tf_op jit(solution)/shard_map/all_to_all | solution.py:111
  362.1 6.4 %all-to-all-start.3 = ((bf16[64,2,8,4096]{3,2,1,0:T(8,128)(2,1)}), bf16[64,2,8,4096]{3,2,1,0:T(8,128)(2,1)}, u32[]{:S(2)}, u32[]{:S(2)}) async-start(bf16[64,2,8,4096]{3,2,1,0:T(8,128)(2,1)} %convolution_convert_fusion), calls=%async_computation.3 | async-start | bytes 16777216 | tf_op jit(solution)/shard_map/all_to_all | solution.py:86
  368.6 6.5 %fusion.2 = f32[128,4096]{1,0:T(8,128)} fusion(bf16[64,2,8,4096]{3,2,1,0:T(8,128)(2,1)} %all-to-all-done, f32[64,2,8,128]{3,2,1,0:T(8,128)} %fusion.7, s32[64,2,8]{2,1,0:T(2,128)S(1)} %get-tuple-element.12, f32[64,2,8]{2,1,0:T(2,128)S(1)} %get-tuple-element.11, f32[64,2,8]{2,1,0:T(2,128)S(1)} %get-tuple-element.10, ...), kind=kOutput, calls=%fused_computation.20 | convolution fusion | flops 1074659328 | bytes 11023360 | tf_op jit(solution)/shard_map/scqw,scqd->wd/dot_general | solution.py:89
  375.0 1.0 scatter_custom_fusion
  376.1 1.5 gather_fusion.5
  377.6 1.7 gather_fusion.7
  379.4 1.6 reduce_sum.75
  380.9 173.3 %all-to-all-done.3 = bf16[64,2,8,4096]{3,2,1,0:T(8,128)(2,1)} async-done(((bf16[64,2,8,4096]{3,2,1,0:T(8,128)(2,1)}), bf16[64,2,8,4096]{3,2,1,0:T(8,128)(2,1)}, u32[]{:S(2)}, u32[]{:S(2)}) %all-to-all-start.3) | async-done | bytes 8388640 | tf_op jit(solution)/shard_map/all_to_all | solution.py:86
  554.2 6.1 %gather_fusion.11 = bf16[64,8,4096]{2,1,0:T(8,128)(2,1)} fusion(bf16[128,8,4096]{2,1,0:T(8,128)(2,1)} %bitcast.24, s32[1024]{0:T(1024)S(1)} %pad_clamp_fusion.2), kind=kCustom, calls=%fused_computation.11 | custom fusion | bytes 8388864 | tf_op jit(solution)/shard_map/gather | solution.py:94
  560.4 3.4 convert_reduce_fusion
  563.8 0.5 fusion.5
  564.2 2.2 gather_fusion.12
  (70 shorter events, 1.2 us)
Async XLA Ops:
  7.2 4.1 copy-start
  19.0 14.2 %copy-start.9 = (s32[64]{0:T(128)S(1)}, s32[64]{0:T(128)}, u32[]{:S(2)}) copy-start(s32[64]{0:T(128)} %param.10) | copy-start | bytes 772
  19.0 15.3 %copy-start.10 = (s32[1,128]{1,0:T(1,128)S(1)}, s32[1,128]{1,0:T(1,128)}, u32[]{:S(2)}) copy-start(s32[1,128]{1,0:T(1,128)} %param.12) | copy-start | bytes 1540
  19.1 15.3 %copy-start.8 = (s32[16,4]{0,1:T(4,128)S(1)}, s32[16,4]{0,1:T(4,128)}, u32[]{:S(2)}) copy-start(s32[16,4]{0,1:T(4,128)} %param.11) | copy-start | bytes 772
  19.1 205.4 %copy-start.6 = (bf16[128,4096]{1,0:T(8,128)(2,1)S(1)}, bf16[128,4096]{1,0:T(8,128)(2,1)}, u32[]{:S(2)}) copy-start(bf16[128,4096]{1,0:T(8,128)(2,1)} %param.8) | copy-start | bytes 3145732
  19.1 205.4 %all-to-all-start = ((bf16[64,2,8,4096]{3,2,1,0:T(8,128)(2,1)}), bf16[64,2,8,4096]{3,2,1,0:T(8,128)(2,1)}, u32[]{:S(2)}, u32[]{:S(2)}) async-start(bf16[64,2,8,4096]{3,2,1,0:T(8,128)(2,1)} %bitcast.78), calls=%async_computation | async-start | bytes 16777216 | tf_op jit(solution)/shard_map/all_to_all | solution.py:44
  32.5 208.6 %all-gather.3.cloned.1.call-start = ((), (), s32[]{:S(2)}) async-start(), calls=%async_computation.9 | async-start | bytes 2129920 | tf_op jit(solution)/shard_map/all_gather | solution.py:24
  230.9 23.4 %all-to-all-start.1 = ((f32[64,2,8,128]{3,2,1,0:T(8,128)}), f32[64,2,8,128]{3,2,1,0:T(8,128)}, u32[]{:S(2)}, u32[]{:S(2)}) async-start(f32[64,2,8,128]{3,2,1,0:T(8,128)} %fusion.7), calls=%async_computation.1 | async-start | bytes 1048576 | tf_op jit(solution)/shard_map/all_to_all | solution.py:48
  237.1 82.4 %reduce-scatter.5.cloned.1.call-start = ((), (), s32[]{:S(2)}) async-start(), calls=%async_computation.8 | async-start | bytes 5242880 | tf_op jit(solution)/shard_map/reduce_scatter | solution.py:110
  237.4 2.2 copy-start.2
  241.1 7.9 %copy-start.5 = (bf16[128,4096]{1,0:T(8,128)(2,1)S(1)}, bf16[128,4096]{1,0:T(8,128)(2,1)}, u32[]{:S(2)}) copy-start(bf16[128,4096]{1,0:T(8,128)(2,1)} %gather_fusion) | copy-start | bytes 3145732
  249.0 12.4 %copy-start.3 = (bf16[256,4096]{1,0:T(8,128)(2,1)}, bf16[256,4096]{1,0:T(8,128)(2,1)S(1)}, u32[]{:S(2)}) copy-start(bf16[256,4096]{1,0:T(8,128)(2,1)S(1)} %reshape.354) | copy-start | bytes 6291460
  273.2 60.6 %copy-start.7 = (bf16[128,4096]{1,0:T(8,128)(2,1)S(1)}, bf16[128,4096]{1,0:T(8,128)(2,1)}, u32[]{:S(2)}) copy-start(bf16[128,4096]{1,0:T(8,128)(2,1)} %param.8) | copy-start | bytes 3145732
  277.2 45.6 %all-to-all-start.2 = ((f32[64,2,8,3]{2,1,3,0:T(2,128)}), f32[64,2,8,3]{2,1,3,0:T(2,128)S(1)}, u32[]{:S(2)}, u32[]{:S(2)}) async-start(f32[64,2,8,3]{2,1,3,0:T(2,128)} %copy.73), calls=%async_computation.2 | async-start | bytes 393216 | tf_op jit(solution)/shard_map/all_to_all | solution.py:73
  322.8 39.3 %all-to-all-start.4 = ((f32[64,1,4096]{2,1,0:T(1,128)}), f32[64,1,4096]{2,1,0:T(1,128)S(1)}, u32[]{:S(2)}, u32[]{:S(2)}) async-start(f32[64,1,4096]{2,1,0:T(1,128)} %copy.78), calls=%async_computation.6 | async-start | bytes 2097152 | tf_op jit(solution)/shard_map/all_to_all | solution.py:111
  362.1 192.1 %all-to-all-start.3 = ((bf16[64,2,8,4096]{3,2,1,0:T(8,128)(2,1)}), bf16[64,2,8,4096]{3,2,1,0:T(8,128)(2,1)}, u32[]{:S(2)}, u32[]{:S(2)}) async-start(bf16[64,2,8,4096]{3,2,1,0:T(8,128)(2,1)} %convolution_convert_fusion), calls=%async_computation.3 | async-start | bytes 16777216 | tf_op jit(solution)/shard_map/all_to_all | solution.py:86
  368.5 197.9 %reduce-scatter.3.cloned.1.call-start = ((), (), s32[]{:S(2)}) async-start(), calls=%async_computation.7 | async-start | bytes 2621440 | tf_op jit(solution)/shard_map/reduce_scatter | solution.py:88
  560.4 3.4 copy-start.4
  563.7 2.7 copy-start.1
Sparse Core Ops, SparseCore 0:
  36.1 92.4 all-gather.2
  273.3 46.2 reduce-scatter.4
  375.2 31.5 reduce-scatter.2

commit v3 on v2

--- a/solution.py
+++ b/solution.py
@@ -11,7 +11,25 @@
 G_DEV = 16
 
 
-def per_device(hidden, cand_embed, freq_embed, owner_order, cand_blocks, group_tokens, target_slot):
+def halving_sum(rows, axis):
+    count = lax.axis_size(axis)
+    depth = count.bit_length() - 1
+    me = lax.axis_index(axis)
+    pieces = rows.reshape((2,) * depth + rows.shape[1:])
+    bits = list(range(depth - 1, -1, -1))
+    order = [0, 1, 4, 2, 5, 3] if depth == 6 else list(range(depth))
+    for bit in order:
+        place = bits.index(bit)
+        mine = (me >> bit) & 1
+        keep = lax.dynamic_index_in_dim(pieces, mine, axis=place, keepdims=False)
+        give = lax.dynamic_index_in_dim(pieces, 1 - mine, axis=place, keepdims=False)
+        pairs = [(i, i ^ (1 << bit)) for i in range(count)]
+        pieces = keep + lax.ppermute(give, axis, pairs)
+        bits.remove(bit)
+    return pieces.reshape((1,) + rows.shape[1:])
+
+
+def per_device_body(hidden, cand_embed, freq_embed, owner_order, cand_blocks, group_tokens, target_slot):
     owners_count = lax.axis_size("vocab")
     token_total = hidden.shape[0]
     freq_count = owners_count * PANEL
@@ -83,6 +101,7 @@
     hidden_part = jnp.einsum(
         "scqw,wd->scqd", prob_here, cand_embed, preferred_element_type=jnp.float32
     ).astype(jnp.bfloat16)
+    hidden_part, prob_late = lax.optimization_barrier((hidden_part, prob_freq))
     parts_home = lax.all_to_all(hidden_part, "vocab", split_axis=0, concat_axis=0, tiled=True)
     window = prob_here
     grad_cand = lax.psum_scatter(
@@ -102,16 +121,16 @@
     embed_columns = (
         position_of[:, None] * PANEL + jnp.arange(PANEL, dtype=jnp.int32)[None, :]
     ).reshape(freq_count)
-    prob_embed = prob_freq[:, embed_columns]
+    token_count = lax.axis_size("token")
+    embed_columns = (
+        embed_columns.reshape(freq_count // token_count, token_count).T.reshape(freq_count)
+    )
+    prob_embed = prob_late[:, embed_columns]
     window = prob_embed
-    token_count = lax.axis_size("token")
     freq_partial = jnp.einsum("tf,td->fd", window, grouped, preferred_element_type=jnp.float32)
-    freq_partial = freq_partial.reshape(freq_count // token_count, token_count, D).transpose(1, 0, 2)
+    freq_partial = freq_partial.reshape(token_count, freq_count // token_count, D)
     freq_partial = lax.psum_scatter(freq_partial, "token", scatter_dimension=0, tiled=True)
-    freq_pieces = lax.all_to_all(
-        freq_partial.reshape(freq_count // token_count, D), "vocab", split_axis=0, concat_axis=0, tiled=True
-    )
-    grad_freq = jnp.sum(freq_pieces, axis=0, keepdims=True)
+    grad_freq = halving_sum(freq_partial.reshape(owners_count, D), "vocab")
     undo = (
         jnp.zeros((token_total,), jnp.int32)
         .at[listing]
@@ -141,5 +160,5 @@
         P(("vocab", "token"), None),
     )
     return jax.shard_map(
-        per_device, mesh=mesh, in_specs=in_specs, out_specs=out_specs, check_vma=False
+        per_device_body, mesh=mesh, in_specs=in_specs, out_specs=out_specs, check_vma=False
     )

time: 574 us -> 529 us (0.922)
  waiting for transfers between devices: 427 us -> 390 us
  local copies, waits for them, and re-layouts: 56.5 us -> 45.8 us
    all_to_all x5 -> x4, waiting for transfers between devices: 390 us -> 204 us  [the longest x1 188 us: per_device_body(): lax.all_to_all(send_rows, 'vocab', split_axis=0, concat_axis=0, tiled=True)]
    ppermute x0 -> x6, waiting for transfers between devices: none -> 144 us  [halving_sum(): pieces = keep + lax.ppermute(give, axis, pairs)]
    ppermute x0 -> x6, starting transfers between devices: none -> 13.2 us  [halving_sum(): pieces = keep + lax.ppermute(give, axis, pairs)]
    reshape x5 -> x3, local copies, waits for them, and re-layouts: 14.5 us -> 2.7 us  [the longest x1 2.54 us: per_device_body(): panels.reshape(owners_count, PANEL, D)[owner_order].reshape(freq_count, D)]
    all_to_all x5 -> x4, starting transfers between devices: 43.1 us -> 31.8 us  [the longest x1 13.5 us: per_device_body(): lax.all_to_all(send_rows, 'vocab', split_axis=0, concat_axis=0, tiled=True)]
  transfers between devices with their start and end apart: 8 -> 13, of which waited for: 5 -> 9; matrix products, arithmetic and copies ran while one was open for 10% -> 10% of each run, Pallas kernels for 0% -> 0%
where the time goes in v3:
time: 529 us; the launch traced here: 528 us
  waiting for transfers between devices  390 us (74%)
  local copies, waits for them, and re-layouts  45.8 us (9%)
  starting transfers between devices  45.3 us (9%)
  matrix products  24.3 us (5%)
  between operations  14.3 us (3%)
  other arithmetic  8.31 us (2%)
    all_to_all x1, waiting for transfers between devices, per_device_body(): lax.all_to_all(send_rows, 'vocab', split_axis=0, concat_axis=0, tiled=True)  188 us
    ppermute x6, waiting for transfers between devices, halving_sum(): pieces = keep + lax.ppermute(give, axis, pairs)  144 us
    reduce_scatter x1, waiting for transfers between devices, per_device_body(): lax.psum_scatter(freq_partial, 'token', scatter_dimension=0, tiled=True)  39.8 us
    all_to_all x1, starting transfers between devices, per_device_body(): lax.all_to_all(send_rows, 'vocab', split_axis=0, concat_axis=0, tiled=True)  13.5 us
    ppermute x6, starting transfers between devices, halving_sum(): pieces = keep + lax.ppermute(give, axis, pairs)  13.2 us
    all_to_all x1, waiting for transfers between devices, per_device_body(): lax.all_to_all(send_stats, 'vocab', split_axis=0, concat_axis=0, tiled=True)  10.6 us
  transfers between devices with their start and end apart: 13, of which 9 were waited for; matrix products, arithmetic and copies ran while one was open for 10% of the time, Pallas kernels for 0%

profile of v3, /device:TPU:1, one launch (start us, length us, event | category | flops | bytes accessed | tf_op | source)
XLA Modules:
  0.0 528.2 jit_solution(16343153282049547397)
XLA Ops:
  7.2 0.5 broadcast.412
  7.7 1.3 reduce.6
  9.1 0.8 copy.46
  10.1 0.2 select_reduce_fusion.2
  10.4 0.7 fusion.17
  11.1 0.6 gather_fusion.2
  11.9 7.8 %gather_fusion.3 = bf16[1024,4096]{1,0:T(8,128)(2,1)} fusion(bf16[128,4096]{1,0:T(8,128)(2,1)S(1)} %copy-done, s32[1024]{0:T(1024)S(1)} %broadcast_clamp_fusion), kind=kCustom, calls=%fused_computation.3 | custom fusion | bytes 16781312 | tf_op jit(solution)/shard_map/gather | solution.py:57
  19.7 13.5 %all-to-all-start = ((bf16[64,2,8,4096]{3,2,1,0:T(8,128)(2,1)}), bf16[64,2,8,4096]{3,2,1,0:T(8,128)(2,1)}, u32[]{:S(2)}, u32[]{:S(2)}) async-start(bf16[64,2,8,4096]{3,2,1,0:T(8,128)(2,1)} %bitcast.100), calls=%async_computation | async-start | bytes 16777216 | tf_op jit(solution)/shard_map/all_to_all | solution.py:62
  33.2 0.7 all-gather.3.cloned.1.call-update
  33.9 0.8 scatter_custom_fusion.1
  35.0 1.2 gather_fusion.6
  36.3 0.7 gather_fusion.10
  37.1 188.0 %all-to-all-done = bf16[64,2,8,4096]{3,2,1,0:T(8,128)(2,1)} async-done(((bf16[64,2,8,4096]{3,2,1,0:T(8,128)(2,1)}), bf16[64,2,8,4096]{3,2,1,0:T(8,128)(2,1)}, u32[]{:S(2)}, u32[]{:S(2)}) %all-to-all-start) | async-done | bytes 8388640 | tf_op jit(solution)/shard_map/all_to_all | solution.py:62
  225.0 6.5 %fusion.7 = f32[64,2,8,128]{3,2,1,0:T(8,128)} fusion(bf16[64,2,8,4096]{3,2,1,0:T(8,128)(2,1)} %all-to-all-done, bf16[128,4096]{1,0:T(8,128)(2,1)S(1)} %copy-done.6), kind=kOutput, calls=%fused_computation.24 | convolution fusion | flops 1073741824 | bytes 9961472 | tf_op jit(solution)/shard_map/scqd,wd->scqw/dot_general | solution.py:63
  231.5 6.2 %all-to-all-start.1 = ((f32[64,2,8,128]{3,2,1,0:T(8,128)}), f32[64,2,8,128]{3,2,1,0:T(8,128)}, u32[]{:S(2)}, u32[]{:S(2)}) async-start(f32[64,2,8,128]{3,2,1,0:T(8,128)} %fusion.7), calls=%async_computation.1 | async-start | bytes 1048576 | tf_op jit(solution)/shard_map/all_to_all | solution.py:66
  237.7 0.1 reduce_sum.64
  237.9 2.2 gather_fusion
  240.0 0.1 gt.19
  240.4 0.2 convert_element_type.61
  240.9 5.3 gather_fusion.1
  246.1 2.5 reshape.353
  248.7 0.9 fusion.25
  249.7 5.2 all-to-all-done.1
  254.9 1.6 gather_fusion.4
  256.8 0.6 gather_fusion.9
  257.5 0.3 fusion.24
  257.8 0.7 gather_fusion.8
  258.6 0.8 copy.56
  259.4 6.3 %all-to-all-start.2 = ((f32[64,2,8,3]{2,1,3,0:T(2,128)}), f32[64,2,8,3]{2,1,3,0:T(2,128)S(1)}, u32[]{:S(2)}, u32[]{:S(2)}) async-start(f32[64,2,8,3]{2,1,3,0:T(2,128)} %copy.56), calls=%async_computation.2 | async-start | bytes 393216 | tf_op jit(solution)/shard_map/all_to_all | solution.py:91
  265.7 0.2 reduce-scatter.5.cloned.1.call-start
  266.0 10.6 %all-to-all-done.2 = f32[64,2,8,3]{2,1,3,0:T(2,128)S(1)} async-done(((f32[64,2,8,3]{2,1,3,0:T(2,128)}), f32[64,2,8,3]{2,1,3,0:T(2,128)S(1)}, u32[]{:S(2)}, u32[]{:S(2)}) %all-to-all-start.2) | async-done | bytes 12320 | tf_op jit(solution)/shard_map/all_to_all | solution.py:91
  276.8 6.1 %convolution_convert_fusion = bf16[64,2,8,4096]{3,2,1,0:T(8,128)(2,1)} fusion(bf16[128,4096]{1,0:T(8,128)(2,1)} %param.8, f32[64,2,8,128]{3,2,1,0:T(8,128)} %fusion.7, s32[64,2,8]{2,1,0:T(2,128)S(1)} %get-tuple-element.20, f32[64,2,8]{2,1,0:T(2,128)S(1)} %get-tuple-element.19, f32[64,2,8]{2,1,0:T(2,128)S(1)} %get-tuple-element.18, ...), kind=kOutput, calls=%fused_computation.19 | convolution fusion | flops 1078853632 | bytes 9974784 | tf_op jit(solution)/shard_map/scqw,wd->scqd/dot_general | solution.py:101
  283.0 0.9 gather_fusion.13
  283.8 3.9 fusion.26
  287.7 5.9 %all-to-all-start.3 = ((bf16[64,2,8,4096]{3,2,1,0:T(8,128)(2,1)}), bf16[64,2,8,4096]{3,2,1,0:T(8,128)(2,1)}, u32[]{:S(2)}, u32[]{:S(2)}) async-start(bf16[64,2,8,4096]{3,2,1,0:T(8,128)(2,1)} %convolution_convert_fusion), calls=%async_computation.3 | async-start | bytes 16777216 | tf_op jit(solution)/shard_map/all_to_all | solution.py:105
  293.7 39.8 %reduce-scatter.5.cloned.1.call-done = f32[1,64,4096]{2,1,0:T(8,128)} async-done(((f32[4,64,4096]{2,1,0:T(8,128)}), f32[1,64,4096]{2,1,0:T(8,128)}) %reduce-scatter.5.cloned.1.call-update) | async-done | bytes 1048592 | tf_op jit(solution)/shard_map/reduce_scatter | solution.py:132
  333.5 1.8 reshape_reshape.3
  335.3 1.1 constant_dynamic-slice_fusion.6
  336.4 0.4 copy.80
  336.8 0.8 collective-permute-start
  337.7 1.5 collective-permute-done
  339.2 0.5 bitcast_add_fusion
  339.8 0.6 constant_dynamic-slice_fusion.4
  340.3 0.2 copy.81
  340.6 1.4 collective-permute-start.1
  341.9 1.0 scatter_custom_fusion
  342.9 138.3 %collective-permute-done.1 = f32[2,2,2,2,4096]{4,3,2,1,0:T(2,128)S(1)} collective-permute-done((f32[2,2,2,2,4096]{4,3,2,1,0:T(2,128)S(1)}, f32[2,2,2,2,4096]{4,3,2,1,0:T(2,128)S(1)}, u32[]{:S(2)}, u32[]{:S(2)}) %collective-permute-start.1) | collective-permute-done | bytes 262176 | tf_op jit(solution)/shard_map/ppermute | solution.py:27
  481.2 0.3 bitcast_add_fusion.1
  481.5 0.8 collective-permute-start.2
  482.3 6.5 %fusion.2 = f32[128,4096]{1,0:T(8,128)} fusion(bf16[64,2,8,4096]{3,2,1,0:T(8,128)(2,1)} %all-to-all-done, f32[64,2,8,128]{3,2,1,0:T(8,128)} %fusion.7, s32[64,2,8]{2,1,0:T(2,128)S(1)} %get-tuple-element.20, f32[64,2,8]{2,1,0:T(2,128)S(1)} %get-tuple-element.19, f32[64,2,8]{2,1,0:T(2,128)S(1)} %get-tuple-element.18, ...), kind=kOutput, calls=%fused_computation.20 | convolution fusion | flops 1074659328 | bytes 11023360 | tf_op jit(solution)/shard_map/scqw,scqd->wd/dot_general | solution.py:108
  488.9 0.1 constant_dynamic-slice_fusion.2
  489.1 2.2 collective-permute-start.3
  491.3 2.6 collective-permute-done.3
  494.0 2.9 collective-permute-start.4
  496.9 1.6 collective-permute-done.4
  498.6 5.1 collective-permute-start.5
  503.7 1.5 gather_fusion.5
  505.3 1.7 gather_fusion.7
  507.0 0.6 add.260
  507.6 6.2 %gather_fusion.11 = bf16[64,8,4096]{2,1,0:T(8,128)(2,1)} fusion(bf16[128,8,4096]{2,1,0:T(8,128)(2,1)} %bitcast.24, s32[1024]{0:T(1024)S(1)} %pad_clamp_fusion.2), kind=kCustom, calls=%fused_computation.11 | custom fusion | bytes 8388864 | tf_op jit(solution)/shard_map/gather | solution.py:113
  513.8 3.4 convert_reduce_fusion
  517.3 0.5 fusion.5
  517.7 2.2 gather_fusion.12
  519.9 1.8 reduce-scatter.3.cloned.1.call-done
  (87 shorter events, 2.8 us)
Async XLA Ops:
  7.2 4.7 copy-start
  19.6 14.2 %copy-start.8 = (s32[64]{0:T(128)S(1)}, s32[64]{0:T(128)}, u32[]{:S(2)}) copy-start(s32[64]{0:T(128)} %param.10) | copy-start | bytes 772
  19.7 15.2 %copy-start.7 = (s32[16,4]{0,1:T(4,128)S(1)}, s32[16,4]{0,1:T(4,128)}, u32[]{:S(2)}) copy-start(s32[16,4]{0,1:T(4,128)} %param.11) | copy-start | bytes 772
  19.7 15.3 %copy-start.2 = (s32[128]{0:T(128)S(1)}, s32[128]{0:T(128)}, u32[]{:S(2)}) copy-start(s32[128]{0:T(128)} %param.13) | copy-start | bytes 1540
  19.7 205.4 %copy-start.6 = (bf16[128,4096]{1,0:T(8,128)(2,1)S(1)}, bf16[128,4096]{1,0:T(8,128)(2,1)}, u32[]{:S(2)}) copy-start(bf16[128,4096]{1,0:T(8,128)(2,1)} %param.8) | copy-start | bytes 3145732
  19.7 205.4 %all-to-all-start = ((bf16[64,2,8,4096]{3,2,1,0:T(8,128)(2,1)}), bf16[64,2,8,4096]{3,2,1,0:T(8,128)(2,1)}, u32[]{:S(2)}, u32[]{:S(2)}) async-start(bf16[64,2,8,4096]{3,2,1,0:T(8,128)(2,1)} %bitcast.100), calls=%async_computation | async-start | bytes 16777216 | tf_op jit(solution)/shard_map/all_to_all | solution.py:62
  33.1 207.7 %all-gather.3.cloned.1.call-start = ((), (), s32[]{:S(2)}) async-start(), calls=%async_computation.8 | async-start | bytes 2129920 | tf_op jit(solution)/shard_map/all_gather | solution.py:42
  231.5 23.4 %all-to-all-start.1 = ((f32[64,2,8,128]{3,2,1,0:T(8,128)}), f32[64,2,8,128]{3,2,1,0:T(8,128)}, u32[]{:S(2)}, u32[]{:S(2)}) async-start(f32[64,2,8,128]{3,2,1,0:T(8,128)} %fusion.7), calls=%async_computation.1 | async-start | bytes 1048576 | tf_op jit(solution)/shard_map/all_to_all | solution.py:66
  240.8 7.8 %copy-start.5 = (bf16[128,4096]{1,0:T(8,128)(2,1)S(1)}, bf16[128,4096]{1,0:T(8,128)(2,1)}, u32[]{:S(2)}) copy-start(bf16[128,4096]{1,0:T(8,128)(2,1)} %gather_fusion) | copy-start | bytes 3145732
  248.7 34.2 %copy-start.3 = (bf16[256,4096]{1,0:T(8,128)(2,1)}, bf16[256,4096]{1,0:T(8,128)(2,1)S(1)}, u32[]{:S(2)}) copy-start(bf16[256,4096]{1,0:T(8,128)(2,1)S(1)} %reshape.353) | copy-start | bytes 6291460
  259.4 17.2 %all-to-all-start.2 = ((f32[64,2,8,3]{2,1,3,0:T(2,128)}), f32[64,2,8,3]{2,1,3,0:T(2,128)S(1)}, u32[]{:S(2)}, u32[]{:S(2)}) async-start(f32[64,2,8,3]{2,1,3,0:T(2,128)} %copy.56), calls=%async_computation.2 | async-start | bytes 393216 | tf_op jit(solution)/shard_map/all_to_all | solution.py:91
  265.7 67.8 %reduce-scatter.5.cloned.1.call-start = ((), (), s32[]{:S(2)}) async-start(), calls=%async_computation.7 | async-start | bytes 5242880 | tf_op jit(solution)/shard_map/reduce_scatter | solution.py:132
  287.7 219.9 %all-to-all-start.3 = ((bf16[64,2,8,4096]{3,2,1,0:T(8,128)(2,1)}), bf16[64,2,8,4096]{3,2,1,0:T(8,128)(2,1)}, u32[]{:S(2)}, u32[]{:S(2)}) async-start(bf16[64,2,8,4096]{3,2,1,0:T(8,128)(2,1)} %convolution_convert_fusion), calls=%async_computation.3 | async-start | bytes 16777216 | tf_op jit(solution)/shard_map/all_to_all | solution.py:105
  293.6 228.1 %reduce-scatter.3.cloned.1.call-start = ((), (), s32[]{:S(2)}) async-start(), calls=%async_computation.6 | async-start | bytes 2621440 | tf_op jit(solution)/shard_map/reduce_scatter | solution.py:107
  336.8 2.4 collective-permute-start
  340.6 140.6 %collective-permute-start.1 = (f32[2,2,2,2,4096]{4,3,2,1,0:T(2,128)S(1)}, f32[2,2,2,2,4096]{4,3,2,1,0:T(2,128)S(1)}, u32[]{:S(2)}, u32[]{:S(2)}) collective-permute-start(f32[2,2,2,2,4096]{4,3,2,1,0:T(2,128)S(1)} %bitcast.106), channel_id=1, source_target_pairs={{0,8},{4,12},{8,0},{12,4},{16,24},{20,28},{24,16},{28,20},{32,40},... | collective-permute-start | bytes 786440 | tf_op jit(solution)/shard_map/ppermute | solution.py:27
  481.5 7.3 %collective-permute-start.2 = (f32[2,2,2,4096]{3,2,1,0:T(2,128)S(1)}, f32[2,2,2,4096]{3,2,1,0:T(2,128)S(1)}, u32[]{:S(2)}, u32[]{:S(2)}) collective-permute-start(f32[2,2,2,4096]{3,2,1,0:T(2,128)S(1)} %dynamic-slice_bitcast_fusion), channel_id=1, source_target_pairs={{0,64},{4,68},{8,72},{12,76},{16,80},{20,84},{24,88},{28,92},{32,9... | collective-permute-start | bytes 393224 | tf_op jit(solution)/shard_map/ppermute | solution.py:27
  489.1 4.8 collective-permute-start.3
  494.0 4.6 collective-permute-start.4
  498.6 8.4 %collective-permute-start.5 = (f32[4096]{0:T(1024)S(1)}, f32[4096]{0:T(1024)S(1)}, u32[]{:S(2)}, u32[]{:S(2)}) collective-permute-start(f32[4096]{0:T(1024)S(1)} %bitcast.114), channel_id=1, source_target_pairs={{0,32},{4,36},{8,40},{12,44},{16,48},{20,52},{24,56},{28,60},{32,0... | collective-permute-start | bytes 49160 | tf_op jit(solution)/shard_map/ppermute | solution.py:27
  513.8 3.4 copy-start.4
  517.3 4.4 copy-start.1
Sparse Core Ops, SparseCore 0:
  36.7 92.4 all-gather.2
  287.9 45.5 reduce-scatter.4
  488.9 32.7 reduce-scatter.2

commit v4 on v3

--- a/solution.py
+++ b/solution.py
@@ -17,7 +17,7 @@
     me = lax.axis_index(axis)
     pieces = rows.reshape((2,) * depth + rows.shape[1:])
     bits = list(range(depth - 1, -1, -1))
-    order = [0, 1, 4, 2, 5, 3] if depth == 6 else list(range(depth))
+    order = [0, 4, 5, 1, 2, 3] if depth == 6 else list(range(depth))
     for bit in order:
         place = bits.index(bit)
         mine = (me >> bit) & 1
@@ -39,8 +39,18 @@
     listing = group_tokens[0]
     grouped = hidden[listing]
     targets = target_slot[listing]
-    panels = lax.all_gather(freq_embed, "vocab", axis=0, tiled=True)
-    freq_table = panels.reshape(owners_count, PANEL, D)[owner_order].reshape(freq_count, D)
+    token_count = lax.axis_size("token")
+    my_row = lax.dynamic_index_in_dim(freq_embed, lax.axis_index("token"), axis=0, keepdims=True)
+    panel_rows = lax.all_gather(my_row, "vocab", axis=0, tiled=True)
+    token_me = lax.axis_index("token")
+    panels = [panel_rows]
+    for shift in range(1, token_count):
+        pairs = [(i, (i + shift) % token_count) for i in range(token_count)]
+        panels.append(lax.ppermute(panel_rows, "token", pairs))
+    panels = jnp.concatenate(panels, axis=0)
+    source_shift = (token_me - jnp.arange(PANEL, dtype=jnp.int32)) % token_count
+    table_rows = (source_shift[None, :] * owners_count + owner_order[:, None]).reshape(freq_count)
+    freq_table = panels[table_rows]
     owner_of = cand_blocks.reshape(requests)
     owner_hot = (owner_of[:, None] == jnp.arange(owners_count, dtype=jnp.int32)[None, :]).astype(
         jnp.int32
@@ -104,8 +114,9 @@
     hidden_part, prob_late = lax.optimization_barrier((hidden_part, prob_freq))
     parts_home = lax.all_to_all(hidden_part, "vocab", split_axis=0, concat_axis=0, tiled=True)
     window = prob_here
+    cand_partial = jnp.einsum("scqw,scqd->wd", window, got_rows, preferred_element_type=jnp.float32)
     grad_cand = lax.psum_scatter(
-        jnp.einsum("scqw,scqd->wd", window, got_rows, preferred_element_type=jnp.float32),
+        cand_partial,
         "token",
         scatter_dimension=0,
         tiled=True,
@@ -113,6 +124,11 @@
     part_rows = parts_home.reshape(slot_count, GTOK, D)[landing].reshape(G_DEV, K, GTOK, D)
     freq_part = jnp.dot(prob_freq, freq_table, preferred_element_type=jnp.float32)
     grad_rows = freq_part + jnp.sum(part_rows, axis=1, dtype=jnp.float32).reshape(token_total, D)
+    undo = (
+        jnp.zeros((token_total,), jnp.int32)
+        .at[listing]
+        .set(jnp.arange(token_total, dtype=jnp.int32))
+    )
     position_of = (
         jnp.zeros((owners_count,), jnp.int32)
         .at[owner_order]
@@ -121,7 +137,6 @@
     embed_columns = (
         position_of[:, None] * PANEL + jnp.arange(PANEL, dtype=jnp.int32)[None, :]
     ).reshape(freq_count)
-    token_count = lax.axis_size("token")
     embed_columns = (
         embed_columns.reshape(freq_count // token_count, token_count).T.reshape(freq_count)
     )
@@ -131,11 +146,6 @@
     freq_partial = freq_partial.reshape(token_count, freq_count // token_count, D)
     freq_partial = lax.psum_scatter(freq_partial, "token", scatter_dimension=0, tiled=True)
     grad_freq = halving_sum(freq_partial.reshape(owners_count, D), "vocab")
-    undo = (
-        jnp.zeros((token_total,), jnp.int32)
-        .at[listing]
-        .set(jnp.arange(token_total, dtype=jnp.int32))
-    )
     logits = all_scores.astype(jnp.bfloat16)[undo]
     loss = token_loss[undo]
     grad_hidden = grad_rows.astype(jnp.bfloat16)[undo]
@@ -159,6 +169,4 @@
         P(("vocab", "token"), None),
         P(("vocab", "token"), None),
     )
-    return jax.shard_map(
-        per_device_body, mesh=mesh, in_specs=in_specs, out_specs=out_specs, check_vma=False
-    )
+    return jax.shard_map(per_device_body, mesh=mesh, in_specs=in_specs, out_specs=out_specs, check_vma=False)

time: 529 us -> 558 us (1.055)
  blocking collectives: 0 us -> 226 us
  waiting for transfers between devices: 390 us -> 190 us
    all_gather x0 -> x1, blocking collectives: none -> 226 us  [per_device_body(): panel_rows = lax.all_gather(my_row, 'vocab', axis=0, tiled=True)]
    all_to_all x1, waiting for transfers between devices: 188 us -> 0.01 us  [per_device_body(): lax.all_to_all(send_rows, 'vocab', split_axis=0, concat_axis=0, tiled=True)]
    ppermute x6, waiting for transfers between devices: 144 us -> 131 us  [halving_sum(): pieces = keep + lax.ppermute(give, axis, pairs)]
  transfers between devices with their start and end apart: 13 -> 15, of which waited for: 9 -> 8; matrix products, arithmetic and copies ran while one was open for 10% -> 9% of each run, Pallas kernels for 0% -> 0%
where the time goes in v4:
time: 558 us; the launch traced here: 556 us
  blocking collectives  226 us (41%)
  waiting for transfers between devices  190 us (34%)
  starting transfers between devices  48.5 us (9%)
  local copies, waits for them, and re-layouts  41.9 us (8%)
  matrix products  24.8 us (4%)
  between operations  14.7 us (3%)
  other arithmetic  9.72 us (2%)
    all_gather x1, blocking collectives, per_device_body(): panel_rows = lax.all_gather(my_row, 'vocab', axis=0, tiled=True)  226 us
    ppermute x6, waiting for transfers between devices, halving_sum(): pieces = keep + lax.ppermute(give, axis, pairs)  131 us
    reduce_scatter x1, waiting for transfers between devices, per_device_body(): lax.psum_scatter(freq_partial, 'token', scatter_dimension=0, tiled=True)  39.2 us
    all_to_all x1, starting transfers between devices, per_device_body(): lax.all_to_all(send_rows, 'vocab', split_axis=0, concat_axis=0, tiled=True)  13.5 us
  transfers between devices with their start and end apart: 15, of which 8 were waited for; matrix products, arithmetic and copies ran while one was open for 9% of the time, Pallas kernels for 0%

profile of v4, /device:TPU:1, one launch (start us, length us, event | category | flops | bytes accessed | tf_op | source)
XLA Modules:
  0.0 556.1 jit_solution(10432644670488963966)
XLA Ops:
  7.2 0.5 broadcast.477
  7.7 1.3 reduce.6
  9.1 0.8 copy.58
  10.1 0.2 select_reduce_fusion.2
  10.4 0.7 fusion.19
  11.1 0.6 gather_fusion.2
  11.9 7.8 %gather_fusion.3 = bf16[1024,4096]{1,0:T(8,128)(2,1)} fusion(bf16[128,4096]{1,0:T(8,128)(2,1)S(1)} %copy-done, s32[1024]{0:T(1024)S(1)} %broadcast_clamp_fusion), kind=kCustom, calls=%fused_computation.3 | custom fusion | bytes 16781312 | tf_op jit(solution)/shard_map/gather | solution.py:67
  19.7 13.5 %all-to-all-start = ((bf16[64,2,8,4096]{3,2,1,0:T(8,128)(2,1)}), bf16[64,2,8,4096]{3,2,1,0:T(8,128)(2,1)}, u32[]{:S(2)}, u32[]{:S(2)}) async-start(bf16[64,2,8,4096]{3,2,1,0:T(8,128)(2,1)} %bitcast.105), calls=%async_computation | async-start | bytes 16777216 | tf_op jit(solution)/shard_map/all_to_all | solution.py:72
  33.2 226.3 %all-gather = bf16[64,1,4096]{2,1,0:T(2,128)(2,1)S(1)} all-gather(bf16[1,1,4096]{2,1,0:T(2,128)(2,1)S(1)} %dynamic-slice_bitcast_fusion.2), channel_id=1, replica_groups=mesh['vocab'=64,'token'=4] {'vocab'}, dimensions={0}, use_global_device_ids=true | all-gather | bytes 532480 | tf_op jit(solution)/shard_map/all_gather | solution.py:44
  259.5 0.6 copy.95
  260.0 2.6 collective-permute-start.2
  262.6 0.5 collective-permute-start.1
  263.1 0.6 collective-permute-start
  263.7 0.1 reduce_sum.64
  263.9 0.8 scatter_custom_fusion.1
  265.2 2.2 gather_fusion
  267.4 1.2 gather_fusion.6
  268.6 0.1 gt.19
  269.0 0.1 convert_element_type.61
  269.3 0.7 gather_fusion.10
  270.1 0.1 iota_compare_fusion.1
  270.3 6.6 %fusion.7 = f32[64,2,8,128]{3,2,1,0:T(8,128)} fusion(bf16[64,2,8,4096]{3,2,1,0:T(8,128)(2,1)} %all-to-all-done, bf16[128,4096]{1,0:T(8,128)(2,1)S(1)} %copy-done.8), kind=kOutput, calls=%fused_computation.25 | convolution fusion | flops 1073741824 | bytes 9961472 | tf_op jit(solution)/shard_map/scqd,wd->scqw/dot_general | solution.py:73
  276.8 9.9 %all-to-all-start.1 = ((f32[64,2,8,128]{3,2,1,0:T(8,128)}), f32[64,2,8,128]{3,2,1,0:T(8,128)}, u32[]{:S(2)}, u32[]{:S(2)}) async-start(f32[64,2,8,128]{3,2,1,0:T(8,128)} %fusion.7), calls=%async_computation.1 | async-start | bytes 1048576 | tf_op jit(solution)/shard_map/all_to_all | solution.py:76
  286.8 0.8 copy-done.9
  287.6 1.7 collective-permute-done
  289.3 1.5 pad_maximum_fusion
  290.8 3.2 gather_fusion.1
  294.0 2.5 fusion.27
  296.6 7.3 %all-to-all-done.1 = f32[64,2,8,128]{3,2,1,0:T(8,128)} async-done(((f32[64,2,8,128]{3,2,1,0:T(8,128)}), f32[64,2,8,128]{3,2,1,0:T(8,128)}, u32[]{:S(2)}, u32[]{:S(2)}) %all-to-all-start.1) | async-done | bytes 524320 | tf_op jit(solution)/shard_map/all_to_all | solution.py:76
  303.9 1.6 gather_fusion.4
  305.8 0.6 gather_fusion.9
  306.5 0.3 fusion.26
  306.8 0.7 gather_fusion.8
  307.6 0.8 copy.68
  308.4 6.3 %all-to-all-start.2 = ((f32[64,2,8,3]{2,1,3,0:T(2,128)}), f32[64,2,8,3]{2,1,3,0:T(2,128)S(1)}, u32[]{:S(2)}, u32[]{:S(2)}) async-start(f32[64,2,8,3]{2,1,3,0:T(2,128)} %copy.68), calls=%async_computation.2 | async-start | bytes 393216 | tf_op jit(solution)/shard_map/all_to_all | solution.py:101
  314.8 10.8 %all-to-all-done.2 = f32[64,2,8,3]{2,1,3,0:T(2,128)S(1)} async-done(((f32[64,2,8,3]{2,1,3,0:T(2,128)}), f32[64,2,8,3]{2,1,3,0:T(2,128)S(1)}, u32[]{:S(2)}, u32[]{:S(2)}) %all-to-all-start.2) | async-done | bytes 12320 | tf_op jit(solution)/shard_map/all_to_all | solution.py:101
  325.8 6.2 %convolution_convert_fusion = bf16[64,2,8,4096]{3,2,1,0:T(8,128)(2,1)} fusion(bf16[128,4096]{1,0:T(8,128)(2,1)} %param.8, f32[64,2,8,128]{3,2,1,0:T(8,128)} %fusion.7, s32[64,2,8]{2,1,0:T(2,128)S(1)} %get-tuple-element.18, f32[64,2,8]{2,1,0:T(2,128)S(1)} %get-tuple-element.17, f32[64,2,8]{2,1,0:T(2,128)S(1)} %get-tuple-element.16, ...), kind=kOutput, calls=%fused_computation.19 | convolution fusion | flops 1078853632 | bytes 9974784 | tf_op jit(solution)/shard_map/scqw,wd->scqd/dot_general | solution.py:111
  332.0 0.9 gather_fusion.13
  332.9 2.7 fusion.28
  335.6 5.9 %all-to-all-start.3 = ((bf16[64,2,8,4096]{3,2,1,0:T(8,128)(2,1)}), bf16[64,2,8,4096]{3,2,1,0:T(8,128)(2,1)}, u32[]{:S(2)}, u32[]{:S(2)}) async-start(bf16[64,2,8,4096]{3,2,1,0:T(8,128)(2,1)} %convolution_convert_fusion), calls=%async_computation.3 | async-start | bytes 16777216 | tf_op jit(solution)/shard_map/all_to_all | solution.py:115
  341.5 39.2 %reduce-scatter.5.cloned.1.call-done = f32[1,64,4096]{2,1,0:T(8,128)} async-done(((f32[4,64,4096]{2,1,0:T(8,128)}), f32[1,64,4096]{2,1,0:T(8,128)}) %reduce-scatter.5.cloned.1.call-update) | async-done | bytes 1048592 | tf_op jit(solution)/shard_map/reduce_scatter | solution.py:147
  380.7 1.8 reshape_reshape.3
  382.5 1.1 constant_dynamic-slice_fusion.6
  383.6 0.4 copy.94
  384.0 0.8 collective-permute-start.3
  384.9 1.5 collective-permute-done.3
  386.4 0.5 bitcast_add_fusion
  387.0 1.5 collective-permute-start.4
  388.5 1.0 scatter_custom_fusion
  389.5 9.8 %collective-permute-done.4 = f32[2,2,2,2,4096]{4,3,2,1,0:T(2,128)S(1)} collective-permute-done((f32[2,2,2,2,4096]{4,3,2,1,0:T(2,128)S(1)}, f32[2,2,2,2,4096]{4,3,2,1,0:T(2,128)S(1)}, u32[]{:S(2)}, u32[]{:S(2)}) %collective-permute-start.4) | collective-permute-done | bytes 262176 | tf_op jit(solution)/shard_map/ppermute | solution.py:27
  399.3 0.1 bitcast_add_fusion.1
  399.5 2.5 collective-permute-start.5
  402.0 6.5 %fusion.2 = f32[128,4096]{1,0:T(8,128)} fusion(bf16[64,2,8,4096]{3,2,1,0:T(8,128)(2,1)} %all-to-all-done, f32[64,2,8,128]{3,2,1,0:T(8,128)} %fusion.7, s32[64,2,8]{2,1,0:T(2,128)S(1)} %get-tuple-element.18, f32[64,2,8]{2,1,0:T(2,128)S(1)} %get-tuple-element.17, f32[64,2,8]{2,1,0:T(2,128)S(1)} %get-tuple-element.16, ...), kind=kOutput, calls=%fused_computation.20 | convolution fusion | flops 1074659328 | bytes 11023360 | tf_op jit(solution)/shard_map/scqw,scqd->wd/dot_general | solution.py:117
  408.6 0.1 constant_dynamic-slice_fusion.4
  408.9 116.0 %collective-permute-done.6 = f32[2,2,4096]{2,1,0:T(2,128)S(1)} collective-permute-done((f32[2,2,4096]{2,1,0:T(2,128)S(1)}, f32[2,2,4096]{2,1,0:T(2,128)S(1)}, u32[]{:S(2)}, u32[]{:S(2)}) %collective-permute-start.6) | collective-permute-done | bytes 65568 | tf_op jit(solution)/shard_map/ppermute | solution.py:27
  525.2 3.6 collective-permute-done.7
  528.9 4.2 collective-permute-start.8
  533.2 1.5 gather_fusion.5
  534.7 1.7 gather_fusion.7
  536.5 0.6 add.314
  537.1 6.1 %gather_fusion.11 = bf16[64,8,4096]{2,1,0:T(8,128)(2,1)} fusion(bf16[128,8,4096]{2,1,0:T(8,128)(2,1)} %bitcast.25, s32[1024]{0:T(1024)S(1)} %pad_clamp_fusion.2), kind=kCustom, calls=%fused_computation.11 | custom fusion | bytes 8388864 | tf_op jit(solution)/shard_map/gather | solution.py:124
  543.2 3.4 convert_reduce_fusion
  546.6 0.5 fusion.5
  547.1 2.2 gather_fusion.12
  (104 shorter events, 3.2 us)
Async XLA Ops:
  7.2 4.7 copy-start
  19.6 13.5 %copy-start.11 = (bf16[4,4096]{1,0:T(4,128)(2,1)S(1)}, bf16[4,4096]{1,0:T(4,128)(2,1)}, u32[]{:S(2)}) copy-start(bf16[4,4096]{1,0:T(4,128)(2,1)} %param.9) | copy-start | bytes 98308
  19.6 244.2 %copy-start.12 = (s32[64]{0:T(128)S(1)}, s32[64]{0:T(128)}, u32[]{:S(2)}) copy-start(s32[64]{0:T(128)} %param.10) | copy-start | bytes 772
  19.6 245.1 %copy-start.10 = (s32[16,4]{0,1:T(4,128)S(1)}, s32[16,4]{0,1:T(4,128)}, u32[]{:S(2)}) copy-start(s32[16,4]{0,1:T(4,128)} %param.11) | copy-start | bytes 772
  19.7 250.6 %all-to-all-start = ((bf16[64,2,8,4096]{3,2,1,0:T(8,128)(2,1)}), bf16[64,2,8,4096]{3,2,1,0:T(8,128)(2,1)}, u32[]{:S(2)}, u32[]{:S(2)}) async-start(bf16[64,2,8,4096]{3,2,1,0:T(8,128)(2,1)} %bitcast.105), calls=%async_computation | async-start | bytes 16777216 | tf_op jit(solution)/shard_map/all_to_all | solution.py:72
  260.0 7.3 %copy-start.6 = (bf16[64,1,4096]{2,0,1:T(8,128)(2,1)}, bf16[64,1,4096]{2,0,1:T(8,128)(2,1)S(1)}, u32[]{:S(2)}) copy-start(bf16[64,1,4096]{2,0,1:T(8,128)(2,1)S(1)} %copy.95) | copy-start | bytes 1572868
  260.0 26.7 %collective-permute-start.2 = (bf16[64,4096]{1,0:T(8,128)(2,1)S(1)}, bf16[64,4096]{1,0:T(8,128)(2,1)S(1)}, u32[]{:S(2)}, u32[]{:S(2)}) collective-permute-start(bf16[64,4096]{1,0:T(8,128)(2,1)S(1)} %bitcast.110), channel_id=1, source_target_pairs={{0,3},{1,0},{2,1},{3,2},{4,7},{5,4},{6,5},{7,6},{8,11},{9,8},{10,9... | collective-permute-start | bytes 1572872 | tf_op jit(solution)/shard_map/ppermute | solution.py:49
  262.6 24.1 %collective-permute-start.1 = (bf16[64,4096]{1,0:T(8,128)(2,1)S(1)}, bf16[64,4096]{1,0:T(8,128)(2,1)}, u32[]{:S(2)}, u32[]{:S(2)}) collective-permute-start(bf16[64,4096]{1,0:T(8,128)(2,1)S(1)} %bitcast.111), channel_id=1, source_target_pairs={{0,2},{1,3},{2,0},{3,1},{4,6},{5,7},{6,4},{7,5},{8,10},{9,11},{10,... | collective-permute-start | bytes 1572872 | tf_op jit(solution)/shard_map/ppermute | solution.py:49
  263.1 26.2 %collective-permute-start = (bf16[64,4096]{1,0:T(8,128)(2,1)S(1)}, bf16[64,4096]{1,0:T(8,128)(2,1)}, u32[]{:S(2)}, u32[]{:S(2)}) collective-permute-start(bf16[64,4096]{1,0:T(8,128)(2,1)S(1)} %bitcast.112), channel_id=1, source_target_pairs={{0,1},{1,2},{2,3},{3,0},{4,5},{5,6},{6,7},{7,4},{8,9},{9,10},{10,1... | collective-permute-start | bytes 1572872 | tf_op jit(solution)/shard_map/ppermute | solution.py:49
  265.2 2.2 copy-start.2
  265.2 5.0 copy-start.8
  270.2 19.1 %copy-start.7 = (bf16[64,1,4096]{2,0,1:T(8,128)(2,1)S(1)}, bf16[64,1,4096]{2,0,1:T(8,128)(2,1)}, u32[]{:S(2)}) copy-start(bf16[64,1,4096]{2,0,1:T(8,128)(2,1)} %copy-done.6) | copy-start | bytes 1572868
  276.8 27.1 %all-to-all-start.1 = ((f32[64,2,8,128]{3,2,1,0:T(8,128)}), f32[64,2,8,128]{3,2,1,0:T(8,128)}, u32[]{:S(2)}, u32[]{:S(2)}) async-start(f32[64,2,8,128]{3,2,1,0:T(8,128)} %fusion.7), calls=%async_computation.1 | async-start | bytes 1048576 | tf_op jit(solution)/shard_map/all_to_all | solution.py:76
  286.7 0.8 copy-start.9
  290.8 3.2 copy-start.4
  308.4 17.2 %all-to-all-start.2 = ((f32[64,2,8,3]{2,1,3,0:T(2,128)}), f32[64,2,8,3]{2,1,3,0:T(2,128)S(1)}, u32[]{:S(2)}, u32[]{:S(2)}) async-start(f32[64,2,8,3]{2,1,3,0:T(2,128)} %copy.68), calls=%async_computation.2 | async-start | bytes 393216 | tf_op jit(solution)/shard_map/all_to_all | solution.py:101
  314.7 66.0 %reduce-scatter.5.cloned.1.call-start = ((), (), s32[]{:S(2)}) async-start(), calls=%async_computation.7 | async-start | bytes 5242880 | tf_op jit(solution)/shard_map/reduce_scatter | solution.py:147
  325.7 7.2 %copy-start.5 = (bf16[128,4096]{1,0:T(8,128)(2,1)S(1)}, bf16[128,4096]{1,0:T(8,128)(2,1)}, u32[]{:S(2)}) copy-start(bf16[128,4096]{1,0:T(8,128)(2,1)} %gather_fusion) | copy-start | bytes 3145732
  335.6 201.5 %all-to-all-start.3 = ((bf16[64,2,8,4096]{3,2,1,0:T(8,128)(2,1)}), bf16[64,2,8,4096]{3,2,1,0:T(8,128)(2,1)}, u32[]{:S(2)}, u32[]{:S(2)}) async-start(bf16[64,2,8,4096]{3,2,1,0:T(8,128)(2,1)} %convolution_convert_fusion), calls=%async_computation.3 | async-start | bytes 16777216 | tf_op jit(solution)/shard_map/all_to_all | solution.py:115
  341.5 207.8 %reduce-scatter.3.cloned.1.call-start = ((), (), s32[]{:S(2)}) async-start(), calls=%async_computation.6 | async-start | bytes 2621440 | tf_op jit(solution)/shard_map/reduce_scatter | solution.py:118
  384.0 2.4 collective-permute-start.3
  387.0 12.3 %collective-permute-start.4 = (f32[2,2,2,2,4096]{4,3,2,1,0:T(2,128)S(1)}, f32[2,2,2,2,4096]{4,3,2,1,0:T(2,128)S(1)}, u32[]{:S(2)}, u32[]{:S(2)}) collective-permute-start(f32[2,2,2,2,4096]{4,3,2,1,0:T(2,128)S(1)} %dynamic-slice_bitcast_fusion), channel_id=1, source_target_pairs={{0,64},{4,68},{8,72},{12,76},{16,80},{20,84},{24,88},{28,92},{32,9... | collective-permute-start | bytes 786440 | tf_op jit(solution)/shard_map/ppermute | solution.py:27
  399.5 9.0 %collective-permute-start.5 = (f32[2,2,2,4096]{3,2,1,0:T(2,128)S(1)}, f32[2,2,2,4096]{3,2,1,0:T(2,128)S(1)}, u32[]{:S(2)}, u32[]{:S(2)}) collective-permute-start(f32[2,2,2,4096]{3,2,1,0:T(2,128)S(1)} %dynamic-slice_bitcast_fusion.1), channel_id=1, source_target_pairs={{0,128},{4,132},{8,136},{12,140},{16,144},{20,148},{24,152},{28,15... | collective-permute-start | bytes 393224 | tf_op jit(solution)/shard_map/ppermute | solution.py:27
  408.7 116.2 %collective-permute-start.6 = (f32[2,2,4096]{2,1,0:T(2,128)S(1)}, f32[2,2,4096]{2,1,0:T(2,128)S(1)}, u32[]{:S(2)}, u32[]{:S(2)}) collective-permute-start(f32[2,2,4096]{2,1,0:T(2,128)S(1)} %bitcast.118), channel_id=1, source_target_pairs={{0,8},{4,12},{8,0},{12,4},{16,24},{20,28},{24,16},{28,20},{32,40},... | collective-permute-start | bytes 196616 | tf_op jit(solution)/shard_map/ppermute | solution.py:27
  525.1 3.8 collective-permute-start.7
  528.9 7.5 %collective-permute-start.8 = (f32[4096]{0:T(1024)S(1)}, f32[4096]{0:T(1024)S(1)}, u32[]{:S(2)}, u32[]{:S(2)}) collective-permute-start(f32[4096]{0:T(1024)S(1)} %bitcast.122), channel_id=1, source_target_pairs={{0,32},{4,36},{8,40},{12,44},{16,48},{20,52},{24,56},{28,60},{32,0... | collective-permute-start | bytes 49160 | tf_op jit(solution)/shard_map/ppermute | solution.py:27
  543.2 3.4 copy-start.3
  546.6 2.7 copy-start.1
Sparse Core Ops, SparseCore 0:
  335.7 44.9 reduce-scatter.4
  408.6 40.9 reduce-scatter.2

commit v5 on v4

--- a/solution.py
+++ b/solution.py
@@ -39,18 +39,8 @@
     listing = group_tokens[0]
     grouped = hidden[listing]
     targets = target_slot[listing]
-    token_count = lax.axis_size("token")
-    my_row = lax.dynamic_index_in_dim(freq_embed, lax.axis_index("token"), axis=0, keepdims=True)
-    panel_rows = lax.all_gather(my_row, "vocab", axis=0, tiled=True)
-    token_me = lax.axis_index("token")
-    panels = [panel_rows]
-    for shift in range(1, token_count):
-        pairs = [(i, (i + shift) % token_count) for i in range(token_count)]
-        panels.append(lax.ppermute(panel_rows, "token", pairs))
-    panels = jnp.concatenate(panels, axis=0)
-    source_shift = (token_me - jnp.arange(PANEL, dtype=jnp.int32)) % token_count
-    table_rows = (source_shift[None, :] * owners_count + owner_order[:, None]).reshape(freq_count)
-    freq_table = panels[table_rows]
+    panels = lax.all_gather(freq_embed, "vocab", axis=0, tiled=True)
+    freq_table = panels.reshape(owners_count, PANEL, D)[owner_order].reshape(freq_count, D)
     owner_of = cand_blocks.reshape(requests)
     owner_hot = (owner_of[:, None] == jnp.arange(owners_count, dtype=jnp.int32)[None, :]).astype(
         jnp.int32
@@ -137,6 +127,7 @@
     embed_columns = (
         position_of[:, None] * PANEL + jnp.arange(PANEL, dtype=jnp.int32)[None, :]
     ).reshape(freq_count)
+    token_count = lax.axis_size("token")
     embed_columns = (
         embed_columns.reshape(freq_count // token_count, token_count).T.reshape(freq_count)
     )

time: 558 us -> 510 us (0.914)
  blocking collectives: 226 us -> 0 us
  waiting for transfers between devices: 190 us -> 375 us
  starting transfers between devices: 48.5 us -> 41.6 us
    all_gather x1 -> x0, blocking collectives: 226 us -> none  [per_device_body(): panel_rows = lax.all_gather(my_row, 'vocab', axis=0, tiled=True)]
    all_to_all x1, waiting for transfers between devices: 0.01 us -> 188 us  [per_device_body(): lax.all_to_all(send_rows, 'vocab', split_axis=0, concat_axis=0, tiled=True)]
  transfers between devices with their start and end apart: 15 -> 13, of which waited for: 8 -> 9; matrix products, arithmetic and copies ran while one was open for 9% -> 10% of each run, Pallas kernels for 0% -> 0%
where the time goes in v5:
time: 510 us; the launch traced here: 508 us
  waiting for transfers between devices  375 us (74%)
  local copies, waits for them, and re-layouts  45 us (9%)
  starting transfers between devices  41.6 us (8%)
  matrix products  24.3 us (5%)
  between operations  14.3 us (3%)
  other arithmetic  8.14 us (2%)
    all_to_all x1, waiting for transfers between devices, per_device_body(): lax.all_to_all(send_rows, 'vocab', split_axis=0, concat_axis=0, tiled=True)  188 us
    ppermute x6, waiting for transfers between devices, halving_sum(): pieces = keep + lax.ppermute(give, axis, pairs)  130 us
    reduce_scatter x1, waiting for transfers between devices, per_device_body(): lax.psum_scatter(freq_partial, 'token', scatter_dimension=0, tiled=True)  39.8 us
    all_to_all x1, starting transfers between devices, per_device_body(): lax.all_to_all(send_rows, 'vocab', split_axis=0, concat_axis=0, tiled=True)  13.5 us
    all_to_all x1, waiting for transfers between devices, per_device_body(): lax.all_to_all(send_stats, 'vocab', split_axis=0, concat_axis=0, tiled=True)  10.6 us
  transfers between devices with their start and end apart: 13, of which 9 were waited for; matrix products, arithmetic and copies ran while one was open for 10% of the time, Pallas kernels for 0%

profile of v5, /device:TPU:1, one launch (start us, length us, event | category | flops | bytes accessed | tf_op | source)
XLA Modules:
  0.0 508.1 jit_solution(4692422397382981012)
XLA Ops:
  7.2 0.5 broadcast.412
  7.7 1.3 reduce.6
  9.1 0.8 copy.46
  10.0 0.1 reduce_window_sum.11
  10.1 0.2 select_reduce_fusion.2
  10.4 0.7 fusion.17
  11.1 0.6 gather_fusion.2
  11.9 7.8 %gather_fusion.3 = bf16[1024,4096]{1,0:T(8,128)(2,1)} fusion(bf16[128,4096]{1,0:T(8,128)(2,1)S(1)} %copy-done, s32[1024]{0:T(1024)S(1)} %broadcast_clamp_fusion), kind=kCustom, calls=%fused_computation.3 | custom fusion | bytes 16781312 | tf_op jit(solution)/shard_map/gather | solution.py:57
  19.7 13.5 %all-to-all-start = ((bf16[64,2,8,4096]{3,2,1,0:T(8,128)(2,1)}), bf16[64,2,8,4096]{3,2,1,0:T(8,128)(2,1)}, u32[]{:S(2)}, u32[]{:S(2)}) async-start(bf16[64,2,8,4096]{3,2,1,0:T(8,128)(2,1)} %bitcast.100), calls=%async_computation | async-start | bytes 16777216 | tf_op jit(solution)/shard_map/all_to_all | solution.py:62
  33.2 0.7 all-gather.3.cloned.1.call-update
  33.9 0.8 scatter_custom_fusion.1
  35.0 1.2 gather_fusion.6
  36.3 0.7 gather_fusion.10
  37.1 188.0 %all-to-all-done = bf16[64,2,8,4096]{3,2,1,0:T(8,128)(2,1)} async-done(((bf16[64,2,8,4096]{3,2,1,0:T(8,128)(2,1)}), bf16[64,2,8,4096]{3,2,1,0:T(8,128)(2,1)}, u32[]{:S(2)}, u32[]{:S(2)}) %all-to-all-start) | async-done | bytes 8388640 | tf_op jit(solution)/shard_map/all_to_all | solution.py:62
  225.0 6.5 %fusion.7 = f32[64,2,8,128]{3,2,1,0:T(8,128)} fusion(bf16[64,2,8,4096]{3,2,1,0:T(8,128)(2,1)} %all-to-all-done, bf16[128,4096]{1,0:T(8,128)(2,1)S(1)} %copy-done.6), kind=kOutput, calls=%fused_computation.24 | convolution fusion | flops 1073741824 | bytes 9961472 | tf_op jit(solution)/shard_map/scqd,wd->scqw/dot_general | solution.py:63
  231.5 6.2 %all-to-all-start.1 = ((f32[64,2,8,128]{3,2,1,0:T(8,128)}), f32[64,2,8,128]{3,2,1,0:T(8,128)}, u32[]{:S(2)}, u32[]{:S(2)}) async-start(f32[64,2,8,128]{3,2,1,0:T(8,128)} %fusion.7), calls=%async_computation.1 | async-start | bytes 1048576 | tf_op jit(solution)/shard_map/all_to_all | solution.py:66
  237.7 0.1 reduce_sum.64
  237.9 2.2 gather_fusion
  240.0 0.1 gt.19
  240.4 0.2 convert_element_type.61
  240.7 0.1 iota_compare_fusion.1
  240.9 5.3 %gather_fusion.1 = bf16[64,4,4096]{2,1,0:T(4,128)(2,1)} fusion(bf16[64,4,4096]{2,1,0:T(4,128)(2,1)} %all-gather.3.cloned.1.call-done, s32[1024]{0:T(1024)S(1)} %pad_clamp_fusion.4), kind=kCustom, calls=%fused_computation.1 | custom fusion | bytes 4194560 | tf_op jit(solution)/shard_map/gather | solution.py:43
  246.1 2.5 reshape.353
  248.7 0.9 fusion.25
  249.7 5.2 %all-to-all-done.1 = f32[64,2,8,128]{3,2,1,0:T(8,128)} async-done(((f32[64,2,8,128]{3,2,1,0:T(8,128)}), f32[64,2,8,128]{3,2,1,0:T(8,128)}, u32[]{:S(2)}, u32[]{:S(2)}) %all-to-all-start.1) | async-done | bytes 524320 | tf_op jit(solution)/shard_map/all_to_all | solution.py:66
  254.9 1.6 gather_fusion.4
  256.6 0.1 reduce_max.29
  256.8 0.6 gather_fusion.9
  257.5 0.3 fusion.24
  257.8 0.7 gather_fusion.8
  258.6 0.8 copy.56
  259.4 6.3 %all-to-all-start.2 = ((f32[64,2,8,3]{2,1,3,0:T(2,128)}), f32[64,2,8,3]{2,1,3,0:T(2,128)S(1)}, u32[]{:S(2)}, u32[]{:S(2)}) async-start(f32[64,2,8,3]{2,1,3,0:T(2,128)} %copy.56), calls=%async_computation.2 | async-start | bytes 393216 | tf_op jit(solution)/shard_map/all_to_all | solution.py:91
  265.7 0.2 reduce-scatter.5.cloned.1.call-start
  266.0 10.6 %all-to-all-done.2 = f32[64,2,8,3]{2,1,3,0:T(2,128)S(1)} async-done(((f32[64,2,8,3]{2,1,3,0:T(2,128)}), f32[64,2,8,3]{2,1,3,0:T(2,128)S(1)}, u32[]{:S(2)}, u32[]{:S(2)}) %all-to-all-start.2) | async-done | bytes 12320 | tf_op jit(solution)/shard_map/all_to_all | solution.py:91
  276.8 6.1 %convolution_convert_fusion = bf16[64,2,8,4096]{3,2,1,0:T(8,128)(2,1)} fusion(bf16[128,4096]{1,0:T(8,128)(2,1)} %param.8, f32[64,2,8,128]{3,2,1,0:T(8,128)} %fusion.7, s32[64,2,8]{2,1,0:T(2,128)S(1)} %get-tuple-element.18, f32[64,2,8]{2,1,0:T(2,128)S(1)} %get-tuple-element.17, f32[64,2,8]{2,1,0:T(2,128)S(1)} %get-tuple-element.16, ...), kind=kOutput, calls=%fused_computation.19 | convolution fusion | flops 1078853632 | bytes 9974784 | tf_op jit(solution)/shard_map/scqw,wd->scqd/dot_general | solution.py:101
  282.9 0.1 copy.59
  283.0 0.9 gather_fusion.13
  283.8 3.9 fusion.26
  287.7 5.9 %all-to-all-start.3 = ((bf16[64,2,8,4096]{3,2,1,0:T(8,128)(2,1)}), bf16[64,2,8,4096]{3,2,1,0:T(8,128)(2,1)}, u32[]{:S(2)}, u32[]{:S(2)}) async-start(bf16[64,2,8,4096]{3,2,1,0:T(8,128)(2,1)} %convolution_convert_fusion), calls=%async_computation.3 | async-start | bytes 16777216 | tf_op jit(solution)/shard_map/all_to_all | solution.py:105
  293.7 39.8 %reduce-scatter.5.cloned.1.call-done = f32[1,64,4096]{2,1,0:T(8,128)} async-done(((f32[4,64,4096]{2,1,0:T(8,128)}), f32[1,64,4096]{2,1,0:T(8,128)}) %reduce-scatter.5.cloned.1.call-update) | async-done | bytes 1048592 | tf_op jit(solution)/shard_map/reduce_scatter | solution.py:138
  333.5 1.8 reshape_reshape.3
  335.3 1.1 constant_dynamic-slice_fusion.6
  336.4 0.4 copy.80
  336.8 0.8 collective-permute-start
  337.7 1.5 collective-permute-done
  339.2 0.5 bitcast_add_fusion
  339.8 1.3 collective-permute-start.1
  341.1 1.0 scatter_custom_fusion
  342.1 9.2 %collective-permute-done.1 = f32[2,2,2,2,4096]{4,3,2,1,0:T(2,128)S(1)} collective-permute-done((f32[2,2,2,2,4096]{4,3,2,1,0:T(2,128)S(1)}, f32[2,2,2,2,4096]{4,3,2,1,0:T(2,128)S(1)}, u32[]{:S(2)}, u32[]{:S(2)}) %collective-permute-start.1) | collective-permute-done | bytes 262176 | tf_op jit(solution)/shard_map/ppermute | solution.py:27
  351.3 0.1 bitcast_add_fusion.1
  351.5 2.9 collective-permute-start.2
  354.4 6.5 %fusion.2 = f32[128,4096]{1,0:T(8,128)} fusion(bf16[64,2,8,4096]{3,2,1,0:T(8,128)(2,1)} %all-to-all-done, f32[64,2,8,128]{3,2,1,0:T(8,128)} %fusion.7, s32[64,2,8]{2,1,0:T(2,128)S(1)} %get-tuple-element.18, f32[64,2,8]{2,1,0:T(2,128)S(1)} %get-tuple-element.17, f32[64,2,8]{2,1,0:T(2,128)S(1)} %get-tuple-element.16, ...), kind=kOutput, calls=%fused_computation.20 | convolution fusion | flops 1074659328 | bytes 11023360 | tf_op jit(solution)/shard_map/scqw,scqd->wd/dot_general | solution.py:107
  360.9 0.2 collective-permute-done.2
  361.2 0.1 constant_dynamic-slice_fusion.4
  361.6 115.6 %collective-permute-done.3 = f32[2,2,4096]{2,1,0:T(2,128)S(1)} collective-permute-done((f32[2,2,4096]{2,1,0:T(2,128)S(1)}, f32[2,2,4096]{2,1,0:T(2,128)S(1)}, u32[]{:S(2)}, u32[]{:S(2)}) %collective-permute-start.3) | collective-permute-done | bytes 65568 | tf_op jit(solution)/shard_map/ppermute | solution.py:27
  477.5 3.6 collective-permute-done.4
  481.2 4.3 collective-permute-start.5
  485.5 1.5 gather_fusion.5
  487.1 1.7 gather_fusion.7
  488.8 0.6 add.260
  489.4 6.1 %gather_fusion.11 = bf16[64,8,4096]{2,1,0:T(8,128)(2,1)} fusion(bf16[128,8,4096]{2,1,0:T(8,128)(2,1)} %bitcast.24, s32[1024]{0:T(1024)S(1)} %pad_clamp_fusion.2), kind=kCustom, calls=%fused_computation.11 | custom fusion | bytes 8388864 | tf_op jit(solution)/shard_map/gather | solution.py:114
  495.6 3.4 convert_reduce_fusion
  499.0 0.5 fusion.5
  499.4 2.2 gather_fusion.12
  (87 shorter events, 2.6 us)
Async XLA Ops:
  7.2 4.7 copy-start
  19.6 14.2 %copy-start.8 = (s32[64]{0:T(128)S(1)}, s32[64]{0:T(128)}, u32[]{:S(2)}) copy-start(s32[64]{0:T(128)} %param.10) | copy-start | bytes 772
  19.7 15.2 %copy-start.7 = (s32[16,4]{0,1:T(4,128)S(1)}, s32[16,4]{0,1:T(4,128)}, u32[]{:S(2)}) copy-start(s32[16,4]{0,1:T(4,128)} %param.11) | copy-start | bytes 772
  19.7 15.3 %copy-start.2 = (s32[128]{0:T(128)S(1)}, s32[128]{0:T(128)}, u32[]{:S(2)}) copy-start(s32[128]{0:T(128)} %param.13) | copy-start | bytes 1540
  19.7 205.4 %copy-start.6 = (bf16[128,4096]{1,0:T(8,128)(2,1)S(1)}, bf16[128,4096]{1,0:T(8,128)(2,1)}, u32[]{:S(2)}) copy-start(bf16[128,4096]{1,0:T(8,128)(2,1)} %param.8) | copy-start | bytes 3145732
  19.7 205.4 %all-to-all-start = ((bf16[64,2,8,4096]{3,2,1,0:T(8,128)(2,1)}), bf16[64,2,8,4096]{3,2,1,0:T(8,128)(2,1)}, u32[]{:S(2)}, u32[]{:S(2)}) async-start(bf16[64,2,8,4096]{3,2,1,0:T(8,128)(2,1)} %bitcast.100), calls=%async_computation | async-start | bytes 16777216 | tf_op jit(solution)/shard_map/all_to_all | solution.py:62
  33.1 207.7 %all-gather.3.cloned.1.call-start = ((), (), s32[]{:S(2)}) async-start(), calls=%async_computation.8 | async-start | bytes 2129920 | tf_op jit(solution)/shard_map/all_gather | solution.py:42
  231.5 23.4 %all-to-all-start.1 = ((f32[64,2,8,128]{3,2,1,0:T(8,128)}), f32[64,2,8,128]{3,2,1,0:T(8,128)}, u32[]{:S(2)}, u32[]{:S(2)}) async-start(f32[64,2,8,128]{3,2,1,0:T(8,128)} %fusion.7), calls=%async_computation.1 | async-start | bytes 1048576 | tf_op jit(solution)/shard_map/all_to_all | solution.py:66
  240.8 7.8 %copy-start.5 = (bf16[128,4096]{1,0:T(8,128)(2,1)S(1)}, bf16[128,4096]{1,0:T(8,128)(2,1)}, u32[]{:S(2)}) copy-start(bf16[128,4096]{1,0:T(8,128)(2,1)} %gather_fusion) | copy-start | bytes 3145732
  248.7 34.2 %copy-start.3 = (bf16[256,4096]{1,0:T(8,128)(2,1)}, bf16[256,4096]{1,0:T(8,128)(2,1)S(1)}, u32[]{:S(2)}) copy-start(bf16[256,4096]{1,0:T(8,128)(2,1)S(1)} %reshape.353) | copy-start | bytes 6291460
  259.4 17.2 %all-to-all-start.2 = ((f32[64,2,8,3]{2,1,3,0:T(2,128)}), f32[64,2,8,3]{2,1,3,0:T(2,128)S(1)}, u32[]{:S(2)}, u32[]{:S(2)}) async-start(f32[64,2,8,3]{2,1,3,0:T(2,128)} %copy.56), calls=%async_computation.2 | async-start | bytes 393216 | tf_op jit(solution)/shard_map/all_to_all | solution.py:91
  265.7 67.8 %reduce-scatter.5.cloned.1.call-start = ((), (), s32[]{:S(2)}) async-start(), calls=%async_computation.7 | async-start | bytes 5242880 | tf_op jit(solution)/shard_map/reduce_scatter | solution.py:138
  287.7 201.7 %all-to-all-start.3 = ((bf16[64,2,8,4096]{3,2,1,0:T(8,128)(2,1)}), bf16[64,2,8,4096]{3,2,1,0:T(8,128)(2,1)}, u32[]{:S(2)}, u32[]{:S(2)}) async-start(bf16[64,2,8,4096]{3,2,1,0:T(8,128)(2,1)} %convolution_convert_fusion), calls=%async_computation.3 | async-start | bytes 16777216 | tf_op jit(solution)/shard_map/all_to_all | solution.py:105
  293.6 208.0 %reduce-scatter.3.cloned.1.call-start = ((), (), s32[]{:S(2)}) async-start(), calls=%async_computation.6 | async-start | bytes 2621440 | tf_op jit(solution)/shard_map/reduce_scatter | solution.py:108
  336.8 2.4 collective-permute-start
  339.8 11.5 %collective-permute-start.1 = (f32[2,2,2,2,4096]{4,3,2,1,0:T(2,128)S(1)}, f32[2,2,2,2,4096]{4,3,2,1,0:T(2,128)S(1)}, u32[]{:S(2)}, u32[]{:S(2)}) collective-permute-start(f32[2,2,2,2,4096]{4,3,2,1,0:T(2,128)S(1)} %dynamic-slice_bitcast_fusion), channel_id=1, source_target_pairs={{0,64},{4,68},{8,72},{12,76},{16,80},{20,84},{24,88},{28,92},{32,9... | collective-permute-start | bytes 786440 | tf_op jit(solution)/shard_map/ppermute | solution.py:27
  351.5 9.7 %collective-permute-start.2 = (f32[2,2,2,4096]{3,2,1,0:T(2,128)S(1)}, f32[2,2,2,4096]{3,2,1,0:T(2,128)S(1)}, u32[]{:S(2)}, u32[]{:S(2)}) collective-permute-start(f32[2,2,2,4096]{3,2,1,0:T(2,128)S(1)} %dynamic-slice_bitcast_fusion.1), channel_id=1, source_target_pairs={{0,128},{4,132},{8,136},{12,140},{16,144},{20,148},{24,152},{28,15... | collective-permute-start | bytes 393224 | tf_op jit(solution)/shard_map/ppermute | solution.py:27
  361.4 115.8 %collective-permute-start.3 = (f32[2,2,4096]{2,1,0:T(2,128)S(1)}, f32[2,2,4096]{2,1,0:T(2,128)S(1)}, u32[]{:S(2)}, u32[]{:S(2)}) collective-permute-start(f32[2,2,4096]{2,1,0:T(2,128)S(1)} %bitcast.109), channel_id=1, source_target_pairs={{0,8},{4,12},{8,0},{12,4},{16,24},{20,28},{24,16},{28,20},{32,40},... | collective-permute-start | bytes 196616 | tf_op jit(solution)/shard_map/ppermute | solution.py:27
  477.4 3.8 collective-permute-start.4
  481.2 7.6 %collective-permute-start.5 = (f32[4096]{0:T(1024)S(1)}, f32[4096]{0:T(1024)S(1)}, u32[]{:S(2)}, u32[]{:S(2)}) collective-permute-start(f32[4096]{0:T(1024)S(1)} %bitcast.114), channel_id=1, source_target_pairs={{0,32},{4,36},{8,40},{12,44},{16,48},{20,52},{24,56},{28,60},{32,0... | collective-permute-start | bytes 49160 | tf_op jit(solution)/shard_map/ppermute | solution.py:27
  495.6 3.4 copy-start.4
  499.0 2.7 copy-start.1
Sparse Core Ops, SparseCore 0:
  36.7 92.4 all-gather.2
  287.9 45.5 reduce-scatter.4
  361.1 40.2 reduce-scatter.2

commit v6 on v5

--- a/solution.py
+++ b/solution.py
@@ -111,14 +111,17 @@
         scatter_dimension=0,
         tiled=True,
     )
-    part_rows = parts_home.reshape(slot_count, GTOK, D)[landing].reshape(G_DEV, K, GTOK, D)
-    freq_part = jnp.dot(prob_freq, freq_table, preferred_element_type=jnp.float32)
-    grad_rows = freq_part + jnp.sum(part_rows, axis=1, dtype=jnp.float32).reshape(token_total, D)
     undo = (
         jnp.zeros((token_total,), jnp.int32)
         .at[listing]
         .set(jnp.arange(token_total, dtype=jnp.int32))
     )
+    flat_index = landing.reshape(G_DEV, K)[undo // GTOK] * GTOK + (undo % GTOK)[:, None]
+    slot_rows = jnp.arange(slot_count * GTOK, dtype=jnp.int32)
+    select = jnp.sum((flat_index[:, :, None] == slot_rows).astype(jnp.bfloat16), axis=1)
+    freq_part = jnp.dot(prob_late[undo], freq_table, preferred_element_type=jnp.float32)
+    parts_flat = parts_home.reshape(slot_count * GTOK, D)
+    grad_rows = freq_part + jnp.dot(select, parts_flat, preferred_element_type=jnp.float32)
     position_of = (
         jnp.zeros((owners_count,), jnp.int32)
         .at[owner_order]
@@ -139,7 +142,7 @@
     grad_freq = halving_sum(freq_partial.reshape(owners_count, D), "vocab")
     logits = all_scores.astype(jnp.bfloat16)[undo]
     loss = token_loss[undo]
-    grad_hidden = grad_rows.astype(jnp.bfloat16)[undo]
+    grad_hidden = grad_rows.astype(jnp.bfloat16)
     return (logits, loss, grad_hidden, grad_cand, grad_freq)
 
 

time: 510 us -> 511 us (level)
  waiting for transfers between devices: 375 us -> 358 us
  matrix products: 24.3 us -> 31.9 us
  other arithmetic: 8.14 us -> 15.6 us
    ppermute x6, waiting for transfers between devices: 130 us -> 117 us  [halving_sum(): pieces = keep + lax.ppermute(give, axis, pairs)]
    gather x2 -> x3, local copies, waits for them, and re-layouts: 8.3 us -> 1.55 us  [the longest x1 0.85 us: per_device_body(): prob_late[undo]]
    dot_general x1 -> x2, matrix products: 0.47 us -> 6.19 us  [the longest x1 4.74 us: per_device_body(): jnp.dot(select, parts_flat, preferred_element_type=jnp.float32)]
  transfers between devices with their start and end apart: 13 -> 13, of which waited for: 9 -> 8; matrix products, arithmetic and copies ran while one was open for 10% -> 12% of each run, Pallas kernels for 0% -> 0%
where the time goes in v6:
time: 511 us; the launch traced here: 510 us
  waiting for transfers between devices  358 us (70%)
  local copies, waits for them, and re-layouts  45.9 us (9%)
  starting transfers between devices  44.3 us (9%)
  matrix products  31.9 us (6%)
  other arithmetic  15.6 us (3%)
  between operations  14.3 us (3%)
    all_to_all x1, waiting for transfers between devices, per_device_body(): lax.all_to_all(send_rows, 'vocab', split_axis=0, concat_axis=0, tiled=True)  188 us
    ppermute x6, waiting for transfers between devices, halving_sum(): pieces = keep + lax.ppermute(give, axis, pairs)  117 us
    reduce_scatter x1, waiting for transfers between devices, per_device_body(): lax.psum_scatter(freq_partial, 'token', scatter_dimension=0, tiled=True)  39.8 us
    all_to_all x1, starting transfers between devices, per_device_body(): lax.all_to_all(send_rows, 'vocab', split_axis=0, concat_axis=0, tiled=True)  13.5 us
    ppermute x6, starting transfers between devices, halving_sum(): pieces = keep + lax.ppermute(give, axis, pairs)  10.9 us
  transfers between devices with their start and end apart: 13, of which 8 were waited for; matrix products, arithmetic and copies ran while one was open for 12% of the time, Pallas kernels for 0%

profile of v6, /device:TPU:1, one launch (start us, length us, event | category | flops | bytes accessed | tf_op | source)
XLA Modules:
  0.0 509.7 jit_solution(7657103592797142449)
XLA Ops:
  7.7 1.3 reduce.7
  9.1 0.8 copy.47
  10.4 0.7 fusion.19
  11.9 7.8 %gather_fusion.3 = bf16[1024,4096]{1,0:T(8,128)(2,1)} fusion(bf16[128,4096]{1,0:T(8,128)(2,1)S(1)} %copy-done, s32[1024]{0:T(1024)S(1)} %broadcast_clamp_fusion), kind=kCustom, calls=%fused_computation.3 | custom fusion | bytes 16781312 | tf_op jit(solution)/shard_map/gather | solution.py:57
  19.7 13.5 %all-to-all-start = ((bf16[64,2,8,4096]{3,2,1,0:T(8,128)(2,1)}), bf16[64,2,8,4096]{3,2,1,0:T(8,128)(2,1)}, u32[]{:S(2)}, u32[]{:S(2)}) async-start(bf16[64,2,8,4096]{3,2,1,0:T(8,128)(2,1)} %bitcast.97), calls=%async_computation | async-start | bytes 16777216 | tf_op jit(solution)/shard_map/all_to_all | solution.py:62
  33.2 0.7 all-gather.3.cloned.1.call-update
  33.9 0.8 scatter_custom_fusion.1
  35.0 1.2 gather_fusion.6
  36.3 0.7 gather_fusion.10
  37.1 187.9 %all-to-all-done = bf16[64,2,8,4096]{3,2,1,0:T(8,128)(2,1)} async-done(((bf16[64,2,8,4096]{3,2,1,0:T(8,128)(2,1)}), bf16[64,2,8,4096]{3,2,1,0:T(8,128)(2,1)}, u32[]{:S(2)}, u32[]{:S(2)}) %all-to-all-start) | async-done | bytes 8388640 | tf_op jit(solution)/shard_map/all_to_all | solution.py:62
  225.0 6.5 %fusion.9 = f32[64,2,8,128]{3,2,1,0:T(8,128)} fusion(bf16[64,2,8,4096]{3,2,1,0:T(8,128)(2,1)} %all-to-all-done, bf16[128,4096]{1,0:T(8,128)(2,1)S(1)} %copy-done.5), kind=kOutput, calls=%fused_computation.26 | convolution fusion | flops 1073741824 | bytes 9961472 | tf_op jit(solution)/shard_map/scqd,wd->scqw/dot_general | solution.py:63
  231.5 6.2 %all-to-all-start.1 = ((f32[64,2,8,128]{3,2,1,0:T(8,128)}), f32[64,2,8,128]{3,2,1,0:T(8,128)}, u32[]{:S(2)}, u32[]{:S(2)}) async-start(f32[64,2,8,128]{3,2,1,0:T(8,128)} %fusion.9), calls=%async_computation.1 | async-start | bytes 1048576 | tf_op jit(solution)/shard_map/all_to_all | solution.py:66
  237.9 2.2 gather_fusion
  240.7 0.8 iota_compare_fusion.2
  241.5 5.2 %gather_fusion.1 = bf16[64,4,4096]{2,1,0:T(4,128)(2,1)} fusion(bf16[64,4,4096]{2,1,0:T(4,128)(2,1)} %all-gather.3.cloned.1.call-done, s32[1024]{0:T(1024)S(1)} %pad_clamp_fusion.5), kind=kCustom, calls=%fused_computation.1 | custom fusion | bytes 4194560 | tf_op jit(solution)/shard_map/gather | solution.py:43
  246.7 2.5 reshape.370
  249.2 2.7 fusion.28
  252.0 2.9 all-to-all-done.1
  254.9 1.6 gather_fusion.4
  256.8 0.6 gather_fusion.9
  257.5 1.9 fusion.27
  259.4 0.7 gather_fusion.8
  260.2 0.8 copy.57
  261.0 7.6 %all-to-all-start.2 = ((f32[64,2,8,3]{2,1,3,0:T(2,128)}), f32[64,2,8,3]{2,1,3,0:T(2,128)}, u32[]{:S(2)}, u32[]{:S(2)}) async-start(f32[64,2,8,3]{2,1,3,0:T(2,128)} %copy.57), calls=%async_computation.2 | async-start | bytes 393216 | tf_op jit(solution)/shard_map/all_to_all | solution.py:91
  268.8 1.0 fusion.14
  269.8 9.6 %all-to-all-done.2 = f32[64,2,8,3]{2,1,3,0:T(2,128)} async-done(((f32[64,2,8,3]{2,1,3,0:T(2,128)}), f32[64,2,8,3]{2,1,3,0:T(2,128)}, u32[]{:S(2)}, u32[]{:S(2)}) %all-to-all-start.2) | async-done | bytes 12320 | tf_op jit(solution)/shard_map/all_to_all | solution.py:91
  279.5 0.9 compare_bitcast_fusion
  280.4 0.9 slice_bitcast_fusion
  281.3 6.1 %convolution_convert_fusion = bf16[64,2,8,4096]{3,2,1,0:T(8,128)(2,1)} fusion(bf16[128,4096]{1,0:T(8,128)(2,1)} %param.8, f32[64,2,8,128]{3,2,1,0:T(8,128)} %fusion.9, s32[64,2,8]{2,1,0:T(2,128)S(1)} %get-tuple-element.18, f32[64,2,8]{2,1,0:T(2,128)S(1)} %get-tuple-element.17, f32[64,2,8]{2,1,0:T(2,128)S(1)} %get-tuple-element.16, ...), kind=kOutput, calls=%fused_computation.18 | convolution fusion | flops 1078853632 | bytes 9974784 | tf_op jit(solution)/shard_map/scqw,wd->scqd/dot_general | solution.py:101
  287.5 0.9 gather_fusion.13
  288.4 3.9 fusion.30
  292.3 5.8 %all-to-all-start.3 = ((bf16[64,2,8,4096]{3,2,1,0:T(8,128)(2,1)}), bf16[64,2,8,4096]{3,2,1,0:T(8,128)(2,1)}, u32[]{:S(2)}, u32[]{:S(2)}) async-start(bf16[64,2,8,4096]{3,2,1,0:T(8,128)(2,1)} %convolution_convert_fusion), calls=%async_computation.3 | async-start | bytes 16777216 | tf_op jit(solution)/shard_map/all_to_all | solution.py:105
  298.2 39.8 %reduce-scatter.5.cloned.1.call-done = f32[1,64,4096]{2,1,0:T(8,128)} async-done(((f32[4,64,4096]{2,1,0:T(8,128)}), f32[1,64,4096]{2,1,0:T(8,128)}) %reduce-scatter.5.cloned.1.call-update) | async-done | bytes 1048592 | tf_op jit(solution)/shard_map/reduce_scatter | solution.py:141
  338.0 2.8 reshape_reshape.3
  340.8 3.5 constant_dynamic-slice_fusion.6
  344.3 1.2 copy.82
  345.5 0.7 collective-permute-start
  346.3 1.1 scatter_custom_fusion
  347.4 0.8 collective-permute-done
  348.2 1.7 bitcast_add_fusion
  349.9 0.8 copy-done.3
  350.7 0.7 dynamic-slice_bitcast_fusion
  351.4 1.2 collective-permute-start.1
  352.7 0.6 gather_fusion.12
  353.4 10.4 %collective-permute-done.1 = f32[2,2,2,2,4096]{4,3,2,1,0:T(2,128)} collective-permute-done((f32[2,2,2,2,4096]{4,3,2,1,0:T(2,128)}, f32[2,2,2,2,4096]{4,3,2,1,0:T(2,128)}, u32[]{:S(2)}, u32[]{:S(2)}) %collective-permute-start.1) | collective-permute-done | bytes 262176 | tf_op jit(solution)/shard_map/ppermute | solution.py:27
  363.8 1.2 bitcast_add_fusion.1
  365.0 0.7 copy-done.6
  365.7 0.7 dynamic-slice_bitcast_fusion.1
  366.3 3.2 collective-permute-start.2
  369.5 6.5 %fusion.2 = f32[128,4096]{1,0:T(8,128)} fusion(bf16[64,2,8,4096]{3,2,1,0:T(8,128)(2,1)} %all-to-all-done, f32[64,2,8,128]{3,2,1,0:T(8,128)} %fusion.9, s32[64,2,8]{2,1,0:T(2,128)S(1)} %get-tuple-element.18, f32[64,2,8]{2,1,0:T(2,128)S(1)} %get-tuple-element.17, f32[64,2,8]{2,1,0:T(2,128)S(1)} %get-tuple-element.16, pred[64,2,8]{2,1,0:T(4,128)(4,1)} %copy-done.8), kind=kOutput, calls=%fused_computation.19 | convolution fusion | flops 1074659328 | bytes 11023360 | tf_op jit(solution)/shard_map/scqw,scqd->wd/dot_general | solution.py:107
  376.0 1.1 bitcast_add_fusion.2
  377.3 1.4 collective-permute-start.3
  378.7 1.0 fusion.7
  379.8 101.9 %collective-permute-done.3 = f32[2,2,4096]{2,1,0:T(2,128)S(1)} collective-permute-done((f32[2,2,4096]{2,1,0:T(2,128)S(1)}, f32[2,2,4096]{2,1,0:T(2,128)S(1)}, u32[]{:S(2)}, u32[]{:S(2)}) %collective-permute-start.3) | collective-permute-done | bytes 65568 | tf_op jit(solution)/shard_map/ppermute | solution.py:27
  482.1 3.6 collective-permute-done.4
  485.8 0.6 constant_dynamic-slice_fusion.7
  486.5 4.1 collective-permute-start.5
  490.6 1.0 fusion.12
  491.6 1.5 gather_fusion.5
  493.1 1.7 gather_fusion.7
  494.8 0.8 gather_fusion.11
  495.7 1.3 add.293
  497.0 4.7 fusion.29
  501.8 1.4 fusion.5
  (95 shorter events, 4.9 us)
Async XLA Ops:
  7.2 4.7 copy-start
  11.1 23.9 %copy-start.9 = (s32[128]{0:T(128)}, s32[128]{0:T(128)S(1)}, u32[]{:S(2)}) copy-start(s32[128]{0:T(128)S(1)} %get-tuple-element.38) | copy-start | bytes 1540
  19.7 14.2 %copy-start.10 = (s32[64]{0:T(128)S(1)}, s32[64]{0:T(128)}, u32[]{:S(2)}) copy-start(s32[64]{0:T(128)} %param.10) | copy-start | bytes 772
  19.7 15.4 %copy-start.1 = (s32[128]{0:T(128)S(1)}, s32[128]{0:T(128)}, u32[]{:S(2)}) copy-start(s32[128]{0:T(128)} %param.13) | copy-start | bytes 1540
  19.7 205.4 %all-to-all-start = ((bf16[64,2,8,4096]{3,2,1,0:T(8,128)(2,1)}), bf16[64,2,8,4096]{3,2,1,0:T(8,128)(2,1)}, u32[]{:S(2)}, u32[]{:S(2)}) async-start(bf16[64,2,8,4096]{3,2,1,0:T(8,128)(2,1)} %bitcast.97), calls=%async_computation | async-start | bytes 16777216 | tf_op jit(solution)/shard_map/all_to_all | solution.py:62
  33.1 191.9 %copy-start.5 = (bf16[128,4096]{1,0:T(8,128)(2,1)S(1)}, bf16[128,4096]{1,0:T(8,128)(2,1)}, u32[]{:S(2)}) copy-start(bf16[128,4096]{1,0:T(8,128)(2,1)} %param.8) | copy-start | bytes 3145732
  33.1 208.3 %all-gather.3.cloned.1.call-start = ((), (), s32[]{:S(2)}) async-start(), calls=%async_computation.8 | async-start | bytes 2129920 | tf_op jit(solution)/shard_map/all_gather | solution.py:42
  231.5 23.4 %all-to-all-start.1 = ((f32[64,2,8,128]{3,2,1,0:T(8,128)}), f32[64,2,8,128]{3,2,1,0:T(8,128)}, u32[]{:S(2)}, u32[]{:S(2)}) async-start(f32[64,2,8,128]{3,2,1,0:T(8,128)} %fusion.9), calls=%async_computation.1 | async-start | bytes 1048576 | tf_op jit(solution)/shard_map/all_to_all | solution.py:66
  256.6 12.3 %copy-start.2 = (f32[64,8,128]{2,1,0:T(8,128)}, f32[64,8,128]{2,1,0:T(8,128)S(1)}, u32[]{:S(2)}) copy-start(f32[64,8,128]{2,1,0:T(8,128)S(1)} %gather_fusion.4) | copy-start | bytes 786436
  261.0 18.5 %all-to-all-start.2 = ((f32[64,2,8,3]{2,1,3,0:T(2,128)}), f32[64,2,8,3]{2,1,3,0:T(2,128)}, u32[]{:S(2)}, u32[]{:S(2)}) async-start(f32[64,2,8,3]{2,1,3,0:T(2,128)} %copy.57), calls=%async_computation.2 | async-start | bytes 393216 | tf_op jit(solution)/shard_map/all_to_all | solution.py:91
  268.6 69.4 %reduce-scatter.5.cloned.1.call-start = ((), (), s32[]{:S(2)}) async-start(), calls=%async_computation.7 | async-start | bytes 5242880 | tf_op jit(solution)/shard_map/reduce_scatter | solution.py:141
  280.4 1.0 copy-start.8
  292.3 204.7 %all-to-all-start.3 = ((bf16[64,2,8,4096]{3,2,1,0:T(8,128)(2,1)}), bf16[64,2,8,4096]{3,2,1,0:T(8,128)(2,1)}, u32[]{:S(2)}, u32[]{:S(2)}) async-start(bf16[64,2,8,4096]{3,2,1,0:T(8,128)(2,1)} %convolution_convert_fusion), calls=%async_computation.3 | async-start | bytes 16777216 | tf_op jit(solution)/shard_map/all_to_all | solution.py:105
  298.1 205.1 %reduce-scatter.3.cloned.1.call-start = ((), (), s32[]{:S(2)}) async-start(), calls=%async_computation.6 | async-start | bytes 2621440 | tf_op jit(solution)/shard_map/reduce_scatter | solution.py:108
  345.5 2.6 collective-permute-start
  349.9 0.8 copy-start.3
  351.4 12.3 %collective-permute-start.1 = (f32[2,2,2,2,4096]{4,3,2,1,0:T(2,128)}, f32[2,2,2,2,4096]{4,3,2,1,0:T(2,128)}, u32[]{:S(2)}, u32[]{:S(2)}) collective-permute-start(f32[2,2,2,2,4096]{4,3,2,1,0:T(2,128)} %dynamic-slice_bitcast_fusion), channel_id=1, source_target_pairs={{0,64},{4,68},{8,72},{12,76},{16,80},{20,84},{24,88},{28,92},{32,9... | collective-permute-start | bytes 786440 | tf_op jit(solution)/shard_map/ppermute | solution.py:27
  365.0 0.7 copy-start.6
  366.3 9.7 %collective-permute-start.2 = (f32[2,2,2,4096]{3,2,1,0:T(2,128)}, f32[2,2,2,4096]{3,2,1,0:T(2,128)S(1)}, u32[]{:S(2)}, u32[]{:S(2)}) collective-permute-start(f32[2,2,2,4096]{3,2,1,0:T(2,128)} %dynamic-slice_bitcast_fusion.1), channel_id=1, source_target_pairs={{0,128},{4,132},{8,136},{12,140},{16,144},{20,148},{24,152},{28,15... | collective-permute-start | bytes 393224 | tf_op jit(solution)/shard_map/ppermute | solution.py:27
  376.0 114.6 %copy-start.4 = (f32[128,256]{1,0:T(8,128)S(1)}, f32[128,256]{1,0:T(8,128)}, u32[]{:S(2)}) copy-start(f32[128,256]{1,0:T(8,128)} %get-tuple-element.37) | copy-start | bytes 393220
  377.3 104.3 %collective-permute-start.3 = (f32[2,2,4096]{2,1,0:T(2,128)S(1)}, f32[2,2,4096]{2,1,0:T(2,128)S(1)}, u32[]{:S(2)}, u32[]{:S(2)}) collective-permute-start(f32[2,2,4096]{2,1,0:T(2,128)S(1)} %bitcast.105), channel_id=1, source_target_pairs={{0,8},{4,12},{8,0},{12,4},{16,24},{20,28},{24,16},{28,20},{32,40},... | collective-permute-start | bytes 196616 | tf_op jit(solution)/shard_map/ppermute | solution.py:27
  481.8 4.0 collective-permute-start.4
  486.5 9.2 %collective-permute-start.5 = (f32[4096]{0:T(1024)}, f32[4096]{0:T(1024)}, u32[]{:S(2)}, u32[]{:S(2)}) collective-permute-start(f32[4096]{0:T(1024)} %bitcast.34), channel_id=1, source_target_pairs={{0,32},{4,36},{8,40},{12,44},{16,48},{20,52},{24,56},{28,60},{32,0... | collective-permute-start | bytes 49160 | tf_op jit(solution)/shard_map/ppermute | solution.py:27
  491.5 4.1 copy-start.7
Sparse Core Ops, SparseCore 0:
  36.7 92.4 all-gather.2
  292.4 45.5 reduce-scatter.4
  376.2 35.8 reduce-scatter.2
